TPU v7x, 128 devices: a whole 4x4x4 slice. The times are simulated.
128 devices in a mesh: feat: 8 (over y, core), dom: 16 (over z, x).
Axes of the slice: x: 4, y: 4, z: 4, core: 2. Of those that a mesh axis runs over, the one named last changes fastest.
Arguments:
- features: bfloat16 [768, 262144], P('feat', 'dom'), may hold values from -6 to 6
- neighbours: int32 [65536, 15], P('dom'), may hold values from 0 to 16383
- self_first: bfloat16 [768, 1024], replicated, may hold values from -0.21875 to 0.21875
- neighbour_first: bfloat16 [768, 1024], replicated, may hold values from -0.21875 to 0.21875
- owners: int32 [655360, 1], P(('feat', 'dom')), may hold values from 0 to 15; in each aligned block of 5120 rows (0 to 5119, 5120 to 10239, ...) at most 400 rows name the same one
- offsets: int32 [65536, 10], P(('feat', 'dom')), may hold values from 0 to 511
- self_second: bfloat16 [1024, 1024], replicated, may hold values from -0.1875 to 0.1875
- neighbour_second: bfloat16 [1024, 1024], replicated, may hold values from -0.1875 to 0.1875
- cotangent: bfloat16 [65536, 1024], P(('feat', 'dom')), may hold values from -0.0234375 to 0.0234375
Outputs:
- second_out: bfloat16 [65536, 1024], P(('feat', 'dom'))
- grad_self_second: float32 [1024, 1024], replicated
- grad_neighbour_second: float32 [1024, 1024], replicated
Inputs may be any that keep to these rules, and one draw needn't show every extreme that they name: `owners`: among the 5120 slots of one device (rows of one device), no partition is named more than 400 times, a bound that some block reaches.
All inputs are finite; a program needn't handle non-finite values.
Results may differ from a plain program's by a relative error of at most 0.007.
Values may be sent and summed in bfloat16 or wider, within the bound.
No kernel may reach another device: no remote copies, remote signals or barrier semaphores. Data moves between devices by JAX's collectives and lax.ppermute only.
A program may use at most 192 MiB of HBM per device.

v0:
```python
import jax
import jax.numpy as jnp
from jax import lax
from jax.sharding import PartitionSpec as P


def contract(left, right):
    return lax.dot_general(
        left, right, (((0,), (0,)), ((), ())), preferred_element_type=jnp.float32
    )


def shards(
    features,
    neighbours,
    self_first,
    neighbour_first,
    owners,
    offsets,
    self_second,
    neighbour_second,
    cotangent,
):
    columns_here = features.shape[0]
    targets_part = neighbours.shape[0]
    fanout_first = neighbours.shape[1]
    hidden_width = self_first.shape[1]
    feat_size = lax.axis_size("feat")
    share_rows = targets_part // feat_size
    gathered = features[:, neighbours.T]
    mixed_rows = (jnp.sum(gathered, axis=1, dtype=jnp.float32) / fanout_first).astype(jnp.bfloat16)
    own_rows = features[:, :targets_part]
    feat_start = lax.axis_index("feat") * columns_here
    weight_self = lax.dynamic_slice_in_dim(self_first, feat_start, columns_here, 0)
    weight_neighbour = lax.dynamic_slice_in_dim(neighbour_first, feat_start, columns_here, 0)
    pre_first = lax.psum_scatter(
        contract(own_rows, weight_self) + contract(mixed_rows, weight_neighbour),
        "feat",
        scatter_dimension=0,
        tiled=True,
    )
    layer_out = jnp.maximum(pre_first, 0.0).astype(jnp.bfloat16)
    seed_rows = cotangent.shape[0]
    fanout_second = offsets.shape[1]
    slot_owner = owners.reshape(-1)
    slot_row = offsets.reshape(-1)
    dom_size = lax.axis_size("dom")
    capacity = 5 * slot_owner.shape[0] // (4 * dom_size)
    onehot = (slot_owner[:, None] == jnp.arange(dom_size, dtype=jnp.int32)[None, :]).astype(
        jnp.int32
    )
    ranking = jnp.sum((jnp.cumsum(onehot, axis=0) - onehot) * onehot, axis=1)
    request_rows = jnp.zeros((dom_size, capacity), jnp.int32).at[slot_owner, ranking].set(slot_row)
    segment = lax.all_gather(layer_out, "dom", axis=0, tiled=True)
    owner_count = segment.shape[0] // share_rows
    local_rows = request_rows + (jnp.arange(owner_count, dtype=jnp.int32) * share_rows)[:, None]
    taken = segment[local_rows]
    fetched = taken[slot_owner, ranking]
    summed = jnp.sum(
        fetched.reshape(seed_rows, fanout_second, hidden_width), axis=1, dtype=jnp.float32
    )
    mean_second = (summed / fanout_second).astype(jnp.bfloat16)
    second_out = (
        jnp.dot(layer_out, self_second, preferred_element_type=jnp.float32)
        + jnp.dot(mean_second, neighbour_second, preferred_element_type=jnp.float32)
    ).astype(jnp.bfloat16)
    grad_self = contract(layer_out, cotangent)
    grad_neighbour = contract(mean_second, cotangent)
    grad_self, grad_neighbour = lax.psum((grad_self, grad_neighbour), ("feat", "dom"))
    return (second_out, grad_self, grad_neighbour)


def solution(mesh):
    placed = (
        P("feat", "dom"),
        P("dom", None),
        P(),
        P(),
        P(("feat", "dom"), None),
        P(("feat", "dom"), None),
        P(),
        P(),
        P(("feat", "dom"), None),
    )
    return jax.shard_map(
        shards,
        mesh=mesh,
        in_specs=placed,
        out_specs=(P(("feat", "dom"), None), P(), P()),
        check_vma=False,
    )
```

profile of v0, /device:TPU:1, one launch (start us, length us, event | category | flops | bytes accessed | tf_op | source)
XLA Modules:
  0.0 846.8 jit_solution(11434361600931771453)
XLA Ops:
  7.2 0.0 copy-start
  7.2 0.0 reduce-scatter.2.cloned.1.call-start
  7.2 0.0 copy-start.5
  7.2 6.0 copy.15
  13.3 0.0 copy-done.5
  13.3 0.1 reshape.55
  13.4 207.0 %gather_fusion = bf16[61440,96]{1,0:T(8,128)(2,1)} fusion(bf16[96,16384]{0,1:T(8,128)(2,1)} %copy.15, s32[61440]{0:T(1024)S(1)} %broadcast_clamp_fusion), kind=kCustom, calls=%fused_computation | custom fusion | bytes 23838720 | tf_op jit(solution)/shard_map/gather | solution.py:30
  220.5 8.2 convert_reduce_fusion
  228.7 0.0 copy-start.1
  228.7 9.5 %fusion.1 = f32[1024,4096]{1,0:T(8,128)} fusion(bf16[96,16384]{1,0:T(8,128)(2,1)} %param.9, bf16[768,1024]{1,0:T(8,128)(2,1)} %param.11, s32[]{:T(128)S(6)} %select_n.26), kind=kOutput, calls=%fused_computation.11 | convolution fusion | flops 805306368 | bytes 17760260 | tf_op jit(solution)/shard_map/dot_general | solution.py:8
  238.1 0.0 copy-done.1
  238.1 14.0 %bitcast_add_fusion = f32[4096,1024]{0,1:T(8,128)} fusion(f32[1024,4096]{1,0:T(8,128)} %fusion.1, f32[4096,96]{1,0:T(8,128)S(1)} %copy-done.1, bf16[768,1024]{1,0:T(8,128)(2,1)} %param.12, s32[]{:T(128)S(6)} %select_n.26), kind=kOutput, calls=%fused_computation.5 | convolution fusion | flops 810287104 | bytes 35323908 | tf_op jit(solution)/shard_map/dot_general | solution.py:8
  252.2 0.0 reduce-scatter.2.cloned.1.call-update
  252.2 0.0 copy-start.6
  252.2 0.0 copy-start.7
  252.2 0.0 all-gather.2.cloned.1.call-start
  252.3 94.5 %reduce-scatter.2.cloned.1.call-done = f32[512,1024]{0,1:T(8,128)} async-done(((f32[4096,1024]{0,1:T(8,128)}), f32[512,1024]{0,1:T(8,128)}) %reduce-scatter.2.cloned.1.call-update) | async-done | bytes 2097168 | tf_op jit(solution)/shard_map/reduce_scatter | solution.py:36
  346.8 2.8 maximum_convert_fusion
  349.6 0.0 copy-start.9
  349.6 0.0 copy-start.8
  349.6 0.0 copy-start.3
  349.6 0.0 all-gather.2.cloned.1.call-update
  349.6 0.0 all-reduce.3.cloned.1.call-start
  349.7 0.0 copy-done.6
  349.7 0.7 fusion.7
  350.5 8.4 reduce-window.6
  358.8 0.5 slice_reduce_fusion
  359.3 0.2 reduce-window.9
  359.5 0.0 copy-done.7
  359.5 0.9 copy.17
  360.4 1.2 reshape.77
  361.5 0.1 broadcast_add_fusion
  361.7 0.1 fusion.6
  361.8 0.1 shift-left_or_fusion
  361.9 0.0 copy-done.9
  361.9 0.1 multiply_reduce_fusion
  362.0 0.0 copy-done.8
  362.0 0.1 and_reduce_fusion
  362.2 19.5 %scatter_custom_fusion = s32[6400]{0:T(1024)S(1)} fusion(s32[5120]{0:T(1024)S(1)} %broadcast_select_fusion, s32[5120]{0:T(1024)S(1)} %reshape.77, s32[]{:T(128)} %constant.16.clone.1), kind=kCustom, calls=%fused_computation.35 | custom fusion | bytes 25604
  381.7 0.1 reshape.51
  381.8 0.1 compare_select_fusion.3
  381.9 0.1 reshape.63
  382.0 0.0 copy-done.3
  382.0 4.5 fusion.18
  386.5 82.1 %all-gather.2.cloned.1.call-done = bf16[8192,1024]{0,1:T(8,128)(2,1)} async-done(((bf16[512,1024]{0,1:T(8,128)(2,1)}), bf16[8192,1024]{0,1:T(8,128)(2,1)}) %all-gather.2.cloned.1.call-update) | async-done | bytes 16777232 | tf_op jit(solution)/shard_map/all_gather | solution.py:54
  468.5 22.4 %copy.18 = bf16[8192,1024]{1,0:T(8,128)(2,1)} copy(bf16[8192,1024]{0,1:T(8,128)(2,1)} %all-gather.2.cloned.1.call-done) | data formatting | bytes 33554432 | tf_op jit(solution)/shard_map/all_gather | solution.py:54
  491.0 36.2 %gather_fusion.1 = bf16[6400,1024]{1,0:T(8,128)(2,1)} fusion(bf16[8192,1024]{1,0:T(8,128)(2,1)} %copy.18, s32[7168]{0:T(1024)S(1)} %pad_clamp_fusion), kind=kCustom, calls=%fused_computation.1 | custom fusion | bytes 26240000 | tf_op jit(solution)/shard_map/gather | solution.py:57
  527.1 101.9 %gather_fusion.2 = bf16[5120,1024]{1,0:T(8,128)(2,1)} fusion(bf16[16,400,1024]{2,1,0:T(8,128)(2,1)} %bitcast.35, s32[5120]{0:T(1024)S(1)} %bitcast.36), kind=kCustom, calls=%fused_computation.2 | custom fusion | bytes 21012480 | tf_op jit(solution)/shard_map/gather | solution.py:58
  629.0 21.4 %reshape.52 = f32[512,10,1024]{2,1,0:T(8,128)} reshape(bf16[5120,1024]{1,0:T(8,128)(2,1)} %gather_fusion.2) | data formatting | bytes 31457280 | tf_op jit(solution)/shard_map/convert_element_type | solution.py:59
  650.4 15.6 %reduce_sum.32 = f32[512,1024]{1,0:T(8,128)} reduce(f32[512,10,1024]{2,1,0:T(8,128)} %reshape.52, f32[]{:T(128)} %constant.8.clone.1), dimensions={1}, to_apply=%region_6.7 | reduce | flops 4718592 | bytes 23068676 | tf_op jit(solution)/shard_map/reduce_sum | solution.py:59
  666.0 5.2 fusion.3
  671.2 0.0 all-reduce.3.cloned.1.call-update
  671.2 0.0 copy-done
  671.2 0.0 copy-start.2
  671.2 0.0 copy-start.10
  671.2 1.3 fusion.17
  672.5 0.3 copy-done.2
  672.8 0.6 copy-done.10
  673.4 2.2 add_convert_fusion
  675.7 157.6 %all-reduce.3.cloned.1.call-done = (f32[1024,1024]{1,0:T(8,128)}, f32[1024,1024]{1,0:T(8,128)}) async-done(((f32[1024,1024]{1,0:T(8,128)}, f32[1024,1024]{1,0:T(8,128)}), (f32[1024,1024]{1,0:T(8,128)}, f32[1024,1024]{1,0:T(8,128)})) %all-reduce.3.cloned.1.call-update) | async-done | bytes 8388624 | tf_op jit(solution)/shard_map/psum | solution.py:69
  833.3 0.0 copy-start.4
  833.3 4.9 copy.24
  838.2 0.0 copy-done.4
  838.2 2.0 copy.25
  (5 shorter events, 0.1 us)
Async XLA Ops:
  7.2 664.0 %copy-start = (bf16[1024,1024]{1,0:T(8,128)(2,1)S(1)}, bf16[1024,1024]{1,0:T(8,128)(2,1)}, u32[]{:S(2)}) copy-start(bf16[1024,1024]{1,0:T(8,128)(2,1)} %param.15) | copy-start | bytes 6291460
  7.2 339.6 %reduce-scatter.2.cloned.1.call-start = ((), (), s32[]{:S(2)}) async-start(), calls=%async_computation.1 | async-start | bytes 18874368 | tf_op jit(solution)/shard_map/reduce_scatter | solution.py:36
  7.2 6.0 copy-start.5
  228.7 9.5 %copy-start.1 = (f32[4096,96]{1,0:T(8,128)S(1)}, f32[4096,96]{1,0:T(8,128)}, u32[]{:S(2)}) copy-start(f32[4096,96]{1,0:T(8,128)} %convert_reduce_fusion) | copy-start | bytes 4718596
  252.2 97.5 %copy-start.6 = (s32[5120,1]{0,1:T(1,128)S(1)}, s32[5120,1]{0,1:T(1,128)}, u32[]{:S(2)}) copy-start(s32[5120,1]{0,1:T(1,128)} %param.13) | copy-start | bytes 61444
  252.2 107.3 %copy-start.7 = (s32[512,10]{0,1:T(8,128)S(1)}, s32[512,10]{0,1:T(8,128)}, u32[]{:S(2)}) copy-start(s32[512,10]{0,1:T(8,128)} %param.14) | copy-start | bytes 61444
  252.2 216.3 %all-gather.2.cloned.1.call-start = ((), (), s32[]{:S(2)}) async-start(), calls=%async_computation.2 | async-start | bytes 17825792 | tf_op jit(solution)/shard_map/all_gather | solution.py:54
  349.6 12.3 %copy-start.9 = (s32[2]{0:T(128)S(1)}, s32[2]{0:T(128)}, u32[]{:S(2)}) copy-start(s32[2]{0:T(128)} %constant.38) | copy-start | bytes 28
  349.6 12.4 %copy-start.8 = (s32[2]{0:T(128)S(1)}, s32[2]{0:T(128)}, u32[]{:S(2)}) copy-start(s32[2]{0:T(128)} %constant.41) | copy-start | bytes 28
  349.6 32.3 %copy-start.3 = (bf16[512,1024]{0,1:T(8,128)(2,1)S(1)}, bf16[512,1024]{0,1:T(8,128)(2,1)}, u32[]{:S(2)}) copy-start(bf16[512,1024]{0,1:T(8,128)(2,1)} %maximum_convert_fusion) | copy-start | bytes 3145732
  349.6 483.6 %all-reduce.3.cloned.1.call-start = ((), (), s32[]{:S(2)}) async-start(), calls=%async_computation.3 | async-start | bytes 16777216 | tf_op jit(solution)/shard_map/psum | solution.py:69
  671.2 1.6 copy-start.2
  671.2 2.2 copy-start.10
  833.3 4.9 copy-start.4
Sparse Core Ops, SparseCore 0:
  252.3 94.4 reduce-scatter.1
  349.8 118.7 all-gather.1
  671.3 161.9 all-reduce.2
where the time goes:
time: 850 us; the launch traced here: 847 us
  local copies, waits for them, and re-layouts  425 us (50%)
  waiting for transfers between devices  334 us (39%)
  other arithmetic  36.7 us (4%)
  matrix products  36.7 us (4%)
  between operations  13.9 us (2%)
    gather x1, local copies, waits for them, and re-layouts, shards(): gathered = features[:, neighbours.T]  207 us
    psum x1, waiting for transfers between devices, shards(): lax.psum((grad_self, grad_neighbour), ('feat', 'dom'))  158 us
    gather x1, local copies, waits for them, and re-layouts, shards(): fetched = taken[slot_owner, ranking]  102 us
    reduce_scatter x1, waiting for transfers between devices, shards(): lax.psum_scatter(contract(own_rows, weight_self) + contract(mixed_rows, w...  94.5 us
    all_gather x1, waiting for transfers between devices, shards(): segment = lax.all_gather(layer_out, 'dom', axis=0, tiled=True)  82.1 us
    gather x1, local copies, waits for them, and re-layouts, shards(): taken = segment[local_rows]  36.2 us
    unnamed x27, local copies, waits for them, and re-layouts  34.2 us
    dot_general x4, matrix products, contract(): lax.dot_general(left, right, (((0,), (0,)), ((), ())), preferred_element_...  33.1 us
  transfers between devices with their start and end apart: 3, of which 3 were waited for; matrix products, arithmetic and copies ran while one was open for 5% of the time, Pallas kernels for 0%

commit v1 on v0

--- a/solution.py
+++ b/solution.py
@@ -27,35 +27,36 @@
     hidden_width = self_first.shape[1]
     feat_size = lax.axis_size("feat")
     share_rows = targets_part // feat_size
-    gathered = features[:, neighbours.T]
-    mixed_rows = (jnp.sum(gathered, axis=1, dtype=jnp.float32) / fanout_first).astype(jnp.bfloat16)
-    own_rows = features[:, :targets_part]
-    feat_start = lax.axis_index("feat") * columns_here
-    weight_self = lax.dynamic_slice_in_dim(self_first, feat_start, columns_here, 0)
-    weight_neighbour = lax.dynamic_slice_in_dim(neighbour_first, feat_start, columns_here, 0)
-    pre_first = lax.psum_scatter(
-        contract(own_rows, weight_self) + contract(mixed_rows, weight_neighbour),
-        "feat",
-        scatter_dimension=0,
-        tiled=True,
+    node_rows = features.T
+    gathered = jnp.take(node_rows, neighbours.reshape(-1), axis=0, mode="clip")
+    mixed_rows = (
+        jnp.sum(
+            gathered.reshape(targets_part, fanout_first, columns_here),
+            axis=1,
+            dtype=jnp.float32,
+        )
+        / fanout_first
+    ).astype(jnp.bfloat16)
+    own_rows = node_rows[:targets_part]
+    both = jnp.stack([own_rows, mixed_rows], axis=1).reshape(
+        feat_size, share_rows, 2, columns_here
     )
+    arrived = lax.all_to_all(both, "feat", 0, 0, tiled=True)
+    lhs = jnp.transpose(arrived, (1, 0, 2, 3)).reshape(share_rows, -1)
+    weights = jnp.stack(
+        [
+            self_first.reshape(feat_size, columns_here, hidden_width),
+            neighbour_first.reshape(feat_size, columns_here, hidden_width),
+        ],
+        axis=1,
+    ).reshape(-1, hidden_width)
+    pre_first = jnp.dot(lhs, weights, preferred_element_type=jnp.float32)
     layer_out = jnp.maximum(pre_first, 0.0).astype(jnp.bfloat16)
     seed_rows = cotangent.shape[0]
     fanout_second = offsets.shape[1]
-    slot_owner = owners.reshape(-1)
-    slot_row = offsets.reshape(-1)
-    dom_size = lax.axis_size("dom")
-    capacity = 5 * slot_owner.shape[0] // (4 * dom_size)
-    onehot = (slot_owner[:, None] == jnp.arange(dom_size, dtype=jnp.int32)[None, :]).astype(
-        jnp.int32
-    )
-    ranking = jnp.sum((jnp.cumsum(onehot, axis=0) - onehot) * onehot, axis=1)
-    request_rows = jnp.zeros((dom_size, capacity), jnp.int32).at[slot_owner, ranking].set(slot_row)
     segment = lax.all_gather(layer_out, "dom", axis=0, tiled=True)
-    owner_count = segment.shape[0] // share_rows
-    local_rows = request_rows + (jnp.arange(owner_count, dtype=jnp.int32) * share_rows)[:, None]
-    taken = segment[local_rows]
-    fetched = taken[slot_owner, ranking]
+    flat_rows = owners.reshape(seed_rows, fanout_second) * share_rows + offsets
+    fetched = jnp.take(segment, flat_rows.reshape(-1), axis=0, mode="clip")
     summed = jnp.sum(
         fetched.reshape(seed_rows, fanout_second, hidden_width), axis=1, dtype=jnp.float32
     )

time: 850 us -> 682 us (0.80)
  local copies, waits for them, and re-layouts: 425 us -> 318 us
  waiting for transfers between devices: 334 us -> 260 us
  blocking collectives: 0 us -> 26.6 us
  matrix products: 36.7 us -> 16 us
    gather x3 -> x2, local copies, waits for them, and re-layouts: 345 us -> 242 us  [the longest x1 208 us: shards(): gathered = jnp.take(node_rows, neighbours.reshape(-1), axis=0, mode='clip')]
    reduce_scatter x1 -> x0, waiting for transfers between devices: 94.5 us -> none  [shards(): lax.psum_scatter(contract(own_rows, weight_self) + contract(mixed_rows, w...]
    all_to_all x0 -> x1, blocking collectives: none -> 26.6 us  [shards(): arrived = lax.all_to_all(both, 'feat', 0, 0, tiled=True)]
    convert_element_type x0 -> x2, local copies, waits for them, and re-layouts: none -> 26.3 us  [the longest x1 26.1 us: shards(): jnp.sum(gathered.reshape(targets_part, fanout_first, columns_here), axis=...]
    dot_general x4 -> x2, matrix products: 33.1 us -> 9.69 us  [contract(): lax.dot_general(left, right, (((0,), (0,)), ((), ())), preferred_element_...]
    all_gather x1 -> x0, local copies, waits for them, and re-layouts: 22.4 us -> none  [shards(): segment = lax.all_gather(layer_out, 'dom', axis=0, tiled=True)]
    all_gather x1, waiting for transfers between devices: 82.1 us -> 103 us  [shards(): segment = lax.all_gather(layer_out, 'dom', axis=0, tiled=True)]
    reduce_sum x2 -> x1, other arithmetic: 8.33 us -> 25.2 us  [shards(): jnp.sum(gathered.reshape(targets_part, fanout_first, columns_here), axis=...]
  transfers between devices with their start and end apart: 3 -> 2, of which waited for: 3 -> 2; matrix products, arithmetic and copies ran while one was open for 5% -> 2% of each run, Pallas kernels for 0% -> 0%
where the time goes in v1:
time: 682 us; the launch traced here: 680 us
  local copies, waits for them, and re-layouts  318 us (47%)
  waiting for transfers between devices  260 us (38%)
  other arithmetic  44.2 us (6%)
  blocking collectives  26.6 us (4%)
  matrix products  16 us (2%)
  between operations  14.2 us (2%)
    gather x1, local copies, waits for them, and re-layouts, shards(): gathered = jnp.take(node_rows, neighbours.reshape(-1), axis=0, mode='clip')  208 us
    psum x1, waiting for transfers between devices, shards(): lax.psum((grad_self, grad_neighbour), ('feat', 'dom'))  157 us
    all_gather x1, waiting for transfers between devices, shards(): segment = lax.all_gather(layer_out, 'dom', axis=0, tiled=True)  103 us
    gather x1, local copies, waits for them, and re-layouts, shards(): fetched = jnp.take(segment, flat_rows.reshape(-1), axis=0, mode='clip')  33.7 us
    all_to_all x1, blocking collectives, shards(): arrived = lax.all_to_all(both, 'feat', 0, 0, tiled=True)  26.6 us
    convert_element_type x1, local copies, waits for them, and re-layouts, shards(): jnp.sum(gathered.reshape(targets_part, fanout_first, columns_here), axis=...  26.1 us
    reduce_sum x1, other arithmetic, shards(): jnp.sum(gathered.reshape(targets_part, fanout_first, columns_here), axis=...  25.2 us
    convert_element_type x1, local copies, waits for them, and re-layouts, shards(): jnp.sum(fetched.reshape(seed_rows, fanout_second, hidden_width), axis=1,...  21.4 us
  transfers between devices with their start and end apart: 2, of which 2 were waited for; matrix products, arithmetic and copies ran while one was open for 2% of the time, Pallas kernels for 0%

profile of v1, /device:TPU:1, one launch (start us, length us, event | category | flops | bytes accessed | tf_op | source)
XLA Modules:
  0.0 679.6 jit_solution(10008456262759413801)
XLA Ops:
  7.2 0.0 copy-start
  7.2 0.0 all-gather.2.cloned.1.call-start
  7.2 3.0 copy.28
  10.3 3.2 reshape.46
  13.5 5.9 copy.26
  19.4 1.3 slice.8
  20.7 1.2 copy.30
  21.9 208.3 %gather_fusion = bf16[61440,96]{1,0:T(8,128)(2,1)} fusion(bf16[16384,96]{1,0:T(8,128)(2,1)} %bitcast.25, s32[61440]{0:T(1024)S(1)} %broadcast_clamp_fusion), kind=kCustom, calls=%fused_computation | custom fusion | bytes 23838720 | tf_op jit(solution)/shard_map/jit(_take)/gather | solution.py:31
  230.3 26.1 %reshape.42 = f32[4096,15,96]{2,1,0:T(8,128)} reshape(bf16[61440,96]{1,0:T(8,128)(2,1)} %gather_fusion) | data formatting | bytes 35389440 | tf_op jit(solution)/shard_map/convert_element_type | solution.py:33
  256.3 25.2 %reduce_sum.18 = f32[4096,96]{1,0:T(8,128)} reduce(f32[4096,15,96]{2,1,0:T(8,128)} %reshape.42, f32[]{:T(128)} %constant.4.clone.1), dimensions={1}, to_apply=%region_0.1 | reduce | flops 5505024 | bytes 25165828 | tf_op jit(solution)/shard_map/reduce_sum | solution.py:33
  281.5 2.8 copy.29
  284.3 1.5 multiply_convert_fusion.1
  285.8 0.0 copy-start.4
  285.8 0.3 copy.36
  286.1 0.2 copy.31
  286.3 0.6 copy-done.4
  286.9 0.1 pad_maximum_fusion
  287.1 0.0 copy-start.8
  287.1 0.0 copy-start.9
  287.1 26.6 %all_to_all.5 = bf16[8,512,2,96]{1,3,2,0:T(8,128)(2,1)S(1)} all-to-all(bf16[8,512,2,96]{1,3,2,0:T(8,128)(2,1)S(1)} %pad_maximum_fusion), channel_id=1, replica_groups=mesh['feat'=8,'dom'=16] {'feat'}, dimensions={0} | all-to-all | bytes 3145728 | tf_op jit(solution)/shard_map/all_to_all | solution.py:44
  313.7 0.0 copy-done.8
  313.7 0.0 copy-done.9
  313.7 0.0 copy-start.6
  313.7 0.0 copy-start.5
  313.7 2.8 fusion.4
  316.5 0.0 copy-start.2
  316.5 0.0 all-gather.2.cloned.1.call-update
  316.5 0.2 all-reduce.3.cloned.1.call-start
  316.8 0.0 copy-done.6
  316.8 0.1 multiply_reduce_fusion
  316.8 0.2 mul.11
  317.1 0.0 copy-done.5
  317.1 0.9 copy.32
  317.9 1.7 add.10
  319.6 1.1 reshape.54
  320.7 0.0 copy-done.2
  320.7 4.5 fusion.13
  325.3 103.3 %all-gather.2.cloned.1.call-done = bf16[8192,1024]{1,0:T(8,128)(2,1)} async-done(((bf16[512,1024]{1,0:T(8,128)(2,1)}), bf16[8192,1024]{1,0:T(8,128)(2,1)}) %all-gather.2.cloned.1.call-update) | async-done | bytes 16777232 | tf_op jit(solution)/shard_map/all_gather | solution.py:57
  428.6 33.7 %gather_fusion.1 = bf16[5120,1024]{1,0:T(8,128)(2,1)} fusion(bf16[8192,1024]{1,0:T(8,128)(2,1)} %all-gather.2.cloned.1.call-done, s32[5120]{0:T(1024)S(1)} %broadcast_clamp_fusion.1), kind=kCustom, calls=%fused_computation.1 | custom fusion | bytes 20992000 | tf_op jit(solution)/shard_map/jit(_take)/gather | solution.py:59
  462.3 21.4 %reshape.43 = f32[512,10,1024]{2,1,0:T(8,128)} reshape(bf16[5120,1024]{1,0:T(8,128)(2,1)} %gather_fusion.1) | data formatting | bytes 31457280 | tf_op jit(solution)/shard_map/convert_element_type | solution.py:60
  483.7 15.6 %reduce_sum.19 = f32[512,1024]{1,0:T(8,128)} reduce(f32[512,10,1024]{2,1,0:T(8,128)} %reshape.43, f32[]{:T(128)} %constant.4.clone.1), dimensions={1}, to_apply=%region_1.2 | reduce | flops 4718592 | bytes 23068676 | tf_op jit(solution)/shard_map/reduce_sum | solution.py:60
  499.3 5.2 fusion.8
  504.5 0.0 all-reduce.3.cloned.1.call-update
  504.5 0.0 copy-done
  504.5 0.0 copy-start.1
  504.5 0.0 copy-start.7
  504.5 1.3 fusion.12
  505.8 0.3 copy-done.1
  506.1 0.6 copy-done.7
  506.7 2.2 add_convert_fusion
  509.0 156.8 %all-reduce.3.cloned.1.call-done = (f32[1024,1024]{1,0:T(8,128)}, f32[1024,1024]{1,0:T(8,128)}) async-done(((f32[1024,1024]{1,0:T(8,128)}, f32[1024,1024]{1,0:T(8,128)}), (f32[1024,1024]{1,0:T(8,128)}, f32[1024,1024]{1,0:T(8,128)})) %all-reduce.3.cloned.1.call-update) | async-done | bytes 8388624 | tf_op jit(solution)/shard_map/psum | solution.py:70
  665.8 0.0 copy-start.3
  665.8 4.9 copy.39
  670.7 0.0 copy-done.3
  670.7 2.0 copy.40
  (2 shorter events, 0.0 us)
Async XLA Ops:
  7.2 497.3 %copy-start = (bf16[1024,1024]{1,0:T(8,128)(2,1)S(1)}, bf16[1024,1024]{1,0:T(8,128)(2,1)}, u32[]{:S(2)}) copy-start(bf16[1024,1024]{1,0:T(8,128)(2,1)} %param.15) | copy-start | bytes 6291460
  7.2 421.4 %all-gather.2.cloned.1.call-start = ((), (), s32[]{:S(2)}) async-start(), calls=%async_computation.1 | async-start | bytes 17825792 | tf_op jit(solution)/shard_map/all_gather | solution.py:57
  285.8 1.1 copy-start.4
  287.1 26.6 %copy-start.8 = (bf16[768,1024]{1,0:T(8,128)(2,1)S(1)}, bf16[768,1024]{1,0:T(8,128)(2,1)}, u32[]{:S(2)}) copy-start(bf16[768,1024]{1,0:T(8,128)(2,1)} %param.12) | copy-start | bytes 4718596
  287.1 26.6 %copy-start.9 = (bf16[768,1024]{1,0:T(8,128)(2,1)S(1)}, bf16[768,1024]{1,0:T(8,128)(2,1)}, u32[]{:S(2)}) copy-start(bf16[768,1024]{1,0:T(8,128)(2,1)} %param.11) | copy-start | bytes 4718596
  313.7 3.1 copy-start.6
  313.7 3.4 copy-start.5
  316.5 4.2 copy-start.2
  316.5 349.3 %all-reduce.3.cloned.1.call-start = ((), (), s32[]{:S(2)}) async-start(), calls=%async_computation.2 | async-start | bytes 16777216 | tf_op jit(solution)/shard_map/psum | solution.py:70
  504.5 1.6 copy-start.1
  504.5 2.2 copy-start.7
  665.8 4.9 copy-start.3
Sparse Core Ops, SparseCore 0:
  316.7 111.9 all-gather.1
  504.6 161.1 all-reduce.2

commit v2 on v1

--- a/solution.py
+++ b/solution.py
@@ -1,6 +1,8 @@
 import jax
 import jax.numpy as jnp
 from jax import lax
+from jax.experimental import pallas as pl
+from jax.experimental.pallas import tpu as pltpu
 from jax.sharding import PartitionSpec as P
 
 
@@ -8,6 +10,35 @@
     return lax.dot_general(
         left, right, (((0,), (0,)), ((), ())), preferred_element_type=jnp.float32
     )
+
+
+def gather_sum(table, index, block=512, unroll=8):
+    count, fanout = index.shape
+    rows, width = table.shape
+
+    def kernel(index_ref, table_ref, out_ref):
+        step = pl.program_id(0)
+
+        def body(t, carry):
+            base = (step * block + t) * fanout
+            acc = table_ref[pl.ds(index_ref[base], 1), :]
+            for k in range(1, fanout):
+                acc = acc + table_ref[pl.ds(index_ref[base + k], 1), :]
+            out_ref[pl.ds(t, 1), :] = acc
+            return carry
+
+        lax.fori_loop(0, block, body, 0, unroll=unroll)
+
+    return pl.pallas_call(
+        kernel,
+        out_shape=jax.ShapeDtypeStruct((count, width), jnp.float32),
+        grid_spec=pltpu.PrefetchScalarGridSpec(
+            num_scalar_prefetch=1,
+            grid=(count // block,),
+            in_specs=[pl.BlockSpec((rows, width), lambda b, i: (0, 0))],
+            out_specs=pl.BlockSpec((block, width), lambda b, i: (b, 0)),
+        ),
+    )(index.reshape(-1), table)
 
 
 def shards(
@@ -28,14 +59,8 @@
     feat_size = lax.axis_size("feat")
     share_rows = targets_part // feat_size
     node_rows = features.T
-    gathered = jnp.take(node_rows, neighbours.reshape(-1), axis=0, mode="clip")
     mixed_rows = (
-        jnp.sum(
-            gathered.reshape(targets_part, fanout_first, columns_here),
-            axis=1,
-            dtype=jnp.float32,
-        )
-        / fanout_first
+        gather_sum(node_rows.astype(jnp.float32), neighbours) / fanout_first
     ).astype(jnp.bfloat16)
     own_rows = node_rows[:targets_part]
     both = jnp.stack([own_rows, mixed_rows], axis=1).reshape(
@@ -56,10 +81,12 @@
     fanout_second = offsets.shape[1]
     segment = lax.all_gather(layer_out, "dom", axis=0, tiled=True)
     flat_rows = owners.reshape(seed_rows, fanout_second) * share_rows + offsets
-    fetched = jnp.take(segment, flat_rows.reshape(-1), axis=0, mode="clip")
-    summed = jnp.sum(
-        fetched.reshape(seed_rows, fanout_second, hidden_width), axis=1, dtype=jnp.float32
+    table_index = jnp.arange(segment.shape[0], dtype=jnp.int32)[None, :]
+    counts = sum(
+        (flat_rows[:, k : k + 1] == table_index).astype(jnp.bfloat16)
+        for k in range(fanout_second)
     )
+    summed = jnp.dot(counts, segment, preferred_element_type=jnp.float32)
     mean_second = (summed / fanout_second).astype(jnp.bfloat16)
     second_out = (
         jnp.dot(layer_out, self_second, preferred_element_type=jnp.float32)

time: 682 us -> 454 us (0.67)
  local copies, waits for them, and re-layouts: 318 us -> 27.7 us
  Pallas kernels: 0 us -> 63.7 us
  other arithmetic: 44.2 us -> 9.53 us
  matrix products: 16 us -> 46.5 us
    gather x2 -> x0, local copies, waits for them, and re-layouts: 242 us -> none  [the longest x1 208 us: shards(): gathered = jnp.take(node_rows, neighbours.reshape(-1), axis=0, mode='clip')]
    pallas_call x0 -> x1, Pallas kernels: none -> 63.7 us  [gather_sum(): pl.pallas_call(kernel, out_shape=jax.ShapeDtypeStruct((count, width), jnp...]
    convert_element_type x3 -> x0, local copies, waits for them, and re-layouts: 47.7 us -> none  [the longest x1 26.1 us: shards(): jnp.sum(gathered.reshape(targets_part, fanout_first, columns_here), axis=...]
    reduce_sum x2 -> x0, other arithmetic: 40.8 us -> none  [the longest x1 25.2 us: shards(): jnp.sum(gathered.reshape(targets_part, fanout_first, columns_here), axis=...]
    dot_general x0 -> x1, matrix products: none -> 32.4 us  [shards(): summed = jnp.dot(counts, segment, preferred_element_type=jnp.float32)]
    unnamed x26 -> x27, local copies, waits for them, and re-layouts: 18.6 us -> 18.3 us
  transfers between devices with their start and end apart: 2 -> 2, of which waited for: 2 -> 2; matrix products, arithmetic and copies ran while one was open for 2% -> 3% of each run, Pallas kernels for 0% -> 0%
where the time goes in v2:
time: 454 us; the launch traced here: 449 us
  waiting for transfers between devices  261 us (57%)
  Pallas kernels  63.7 us (14%)
  matrix products  46.5 us (10%)
  local copies, waits for them, and re-layouts  27.7 us (6%)
  blocking collectives  26.3 us (6%)
  between operations  14.6 us (3%)
  other arithmetic  9.53 us (2%)
    psum x1, waiting for transfers between devices, shards(): lax.psum((grad_self, grad_neighbour), ('feat', 'dom'))  157 us
    all_gather x1, waiting for transfers between devices, shards(): segment = lax.all_gather(layer_out, 'dom', axis=0, tiled=True)  104 us
    pallas_call x1, Pallas kernels, gather_sum(): pl.pallas_call(kernel, out_shape=jax.ShapeDtypeStruct((count, width), jnp...  63.7 us
    dot_general x1, matrix products, shards(): summed = jnp.dot(counts, segment, preferred_element_type=jnp.float32)  32.4 us
    all_to_all x1, blocking collectives, shards(): arrived = lax.all_to_all(both, 'feat', 0, 0, tiled=True)  26.3 us
    unnamed x27, local copies, waits for them, and re-layouts  18.3 us
  transfers between devices with their start and end apart: 2, of which 2 were waited for; matrix products, arithmetic and copies ran while one was open for 3% of the time, Pallas kernels for 0%

profile of v2, /device:TPU:1, one launch (start us, length us, event | category | flops | bytes accessed | tf_op | source)
XLA Modules:
  0.0 449.4 jit_solution(6167250339207468222)
XLA Ops:
  7.2 0.0 copy-start
  7.2 0.0 all-gather.2.cloned.1.call-start
  7.2 3.0 copy.21
  10.3 3.9 reshape.19.index_ref
  14.2 5.9 %copy.20 = bf16[96,16384]{0,1:T(8,128)(2,1)} copy(bf16[96,16384]{1,0:T(8,128)(2,1)} %param.9) | data formatting | bytes 6291456 | tf_op args[0]
  20.0 5.1 %bitcast_convert_fusion.table_ref = f32[16384,96]{1,0:T(8,128)} fusion(bf16[96,16384]{0,1:T(8,128)(2,1)} %copy.20), kind=kLoop, calls=%fused_computation.63 | loop fusion | flops 1572864 | bytes 9437184 | tf_op jit(solution)/shard_map/convert_element_type | solution.py:63
  25.1 1.3 slice.44
  26.4 1.2 copy.22
  27.7 63.7 %shard_map.112 = f32[4096,96]{1,0:T(8,128)} custom-call(s32[61440]{0:T(1024)} %reshape.19.index_ref, f32[16384,96]{1,0:T(8,128)} %bitcast_convert_fusion.table_ref), custom_call_target="tpu_custom_call" | custom-call | tf_op jit(solution)/shard_map/pallas_call | solution.py:32
  91.4 1.8 multiply_convert_fusion.1
  93.1 1.2 copy.23
  94.4 0.0 copy-start.9
  94.4 0.0 copy-start.10
  94.4 1.7 pad_maximum_fusion
  96.0 26.3 %all_to_all.5 = bf16[8,512,2,96]{1,3,2,0:T(8,128)(2,1)S(1)} all-to-all(bf16[8,512,2,96]{1,3,2,0:T(8,128)(2,1)S(1)} %pad_maximum_fusion), channel_id=1, replica_groups=mesh['feat'=8,'dom'=16] {'feat'}, dimensions={0} | all-to-all | bytes 3145728 | tf_op jit(solution)/shard_map/all_to_all | solution.py:69
  122.3 0.0 copy-done.9
  122.4 0.0 copy-done.10
  122.4 0.0 copy-start.7
  122.4 0.0 copy-start.6
  122.4 2.8 fusion.44
  125.2 0.0 copy-start.1
  125.2 0.0 all-gather.2.cloned.1.call-update
  125.2 0.2 all-reduce.3.cloned.1.call-start
  125.4 0.0 copy-done.7
  125.4 0.1 multiply_reduce_fusion
  125.5 0.2 mul.11
  125.7 0.0 copy-done.6
  125.7 0.9 copy.24
  126.6 1.0 add.37
  127.5 1.4 slice_reduce_fusion.9
  128.9 0.0 copy-done.1
  128.9 4.5 %fusion.52 = f32[1024,1024]{1,0:T(8,128)} fusion(bf16[512,1024]{1,0:T(8,128)(2,1)S(1)} %copy-done.1, bf16[512,1024]{1,0:T(8,128)(2,1)} %param.17), kind=kOutput, calls=%fused_computation.65 | convolution fusion | flops 1073741824 | bytes 6291456 | tf_op jit(solution)/shard_map/dot_general | solution.py:10
  133.5 103.7 %all-gather.2.cloned.1.call-done = bf16[8192,1024]{1,0:T(8,128)(2,1)} async-done(((bf16[512,1024]{1,0:T(8,128)(2,1)}), bf16[8192,1024]{1,0:T(8,128)(2,1)}) %all-gather.2.cloned.1.call-update) | async-done | bytes 16777232 | tf_op jit(solution)/shard_map/all_gather | solution.py:82
  237.2 0.0 copy-start.3
  237.2 32.4 %multiply_convert_fusion = bf16[512,1024]{1,0:T(8,128)(2,1)S(1)} fusion(bf16[8192,1024]{1,0:T(8,128)(2,1)} %all-gather.2.cloned.1.call-done, s32[512]{0:T(512)S(1)} %get-tuple-element.4, s32[512]{0:T(512)S(1)} %get-tuple-element.5, s32[512]{0:T(512)S(1)} %get-tuple-element.6, s32[512]{0:T(512)S(1)} %get-tuple-element.7, s32[512]{0:T(512)S(1)} %get-tuple-element.8, ...), kind=kOutput, calls=%fused_computation.47 | convolution fusion | flops 8758755328 | bytes 17846272 | tf_op jit(solution)/shard_map/dot_general | solution.py:89
  269.6 0.0 copy-start.4
  269.6 1.0 copy-done.4
  270.6 0.0 copy-done.3
  270.6 3.3 fusion.53
  273.9 0.0 all-reduce.3.cloned.1.call-update
  273.9 0.0 copy-done
  273.9 0.0 copy-start.5
  273.9 0.0 copy-start.8
  273.9 1.2 fusion.51
  275.2 0.0 copy-done.5
  275.2 0.6 copy-done.8
  275.8 2.2 add_convert_fusion
  278.1 157.1 %all-reduce.3.cloned.1.call-done = (f32[1024,1024]{1,0:T(8,128)}, f32[1024,1024]{1,0:T(8,128)}) async-done(((f32[1024,1024]{1,0:T(8,128)}, f32[1024,1024]{1,0:T(8,128)}), (f32[1024,1024]{1,0:T(8,128)}, f32[1024,1024]{1,0:T(8,128)})) %all-reduce.3.cloned.1.call-update) | async-done | bytes 8388624 | tf_op jit(solution)/shard_map/psum | solution.py:97
  435.2 0.0 copy-start.2
  435.2 4.9 %copy.28 = f32[1024,1024]{1,0:T(8,128)} copy(f32[1024,1024]{1,0:T(8,128)} %get-tuple-element.16) | data formatting | bytes 8388608
  440.1 0.0 copy-done.2
  440.1 2.0 copy.29
Async XLA Ops:
  7.2 266.7 %copy-start = (bf16[1024,1024]{1,0:T(8,128)(2,1)S(1)}, bf16[1024,1024]{1,0:T(8,128)(2,1)}, u32[]{:S(2)}) copy-start(bf16[1024,1024]{1,0:T(8,128)(2,1)} %param.15) | copy-start | bytes 6291460
  7.2 230.0 %all-gather.2.cloned.1.call-start = ((), (), s32[]{:S(2)}) async-start(), calls=%async_computation.1 | async-start | bytes 17825792 | tf_op jit(solution)/shard_map/all_gather | solution.py:82
  94.4 28.0 %copy-start.9 = (bf16[768,1024]{1,0:T(8,128)(2,1)S(1)}, bf16[768,1024]{1,0:T(8,128)(2,1)}, u32[]{:S(2)}) copy-start(bf16[768,1024]{1,0:T(8,128)(2,1)} %param.12) | copy-start | bytes 4718596
  94.4 28.0 %copy-start.10 = (bf16[768,1024]{1,0:T(8,128)(2,1)S(1)}, bf16[768,1024]{1,0:T(8,128)(2,1)}, u32[]{:S(2)}) copy-start(bf16[768,1024]{1,0:T(8,128)(2,1)} %param.11) | copy-start | bytes 4718596
  122.4 3.1 copy-start.7
  122.4 3.3 copy-start.6
  125.2 3.8 copy-start.1
  125.2 310.0 %all-reduce.3.cloned.1.call-start = ((), (), s32[]{:S(2)}) async-start(), calls=%async_computation.2 | async-start | bytes 16777216 | tf_op jit(solution)/shard_map/psum | solution.py:97
  237.2 33.4 %copy-start.3 = (bf16[512,1024]{1,0:T(8,128)(2,1)S(1)}, bf16[512,1024]{1,0:T(8,128)(2,1)}, u32[]{:S(2)}) copy-start(bf16[512,1024]{1,0:T(8,128)(2,1)} %param.17) | copy-start | bytes 3145732
  269.6 1.0 copy-start.4
  273.9 1.3 copy-start.5
  273.9 1.9 copy-start.8
  435.2 4.9 %copy-start.2 = (f32[1024,1024]{1,0:T(8,128)S(1)}, f32[1024,1024]{1,0:T(8,128)}, u32[]{:S(2)}) copy-start(f32[1024,1024]{1,0:T(8,128)} %get-tuple-element.17) | copy-start | bytes 12582916
Sparse Core Ops, SparseCore 0:
  125.3 111.8 all-gather.1
  274.0 161.1 all-reduce.2

commit v3 on v2

--- a/solution.py
+++ b/solution.py
@@ -13,17 +13,17 @@
 
 
 def gather_sum(table, index, block=512, unroll=8):
-    count, fanout = index.shape
+    fanout, count = index.shape
     rows, width = table.shape
 
     def kernel(index_ref, table_ref, out_ref):
         step = pl.program_id(0)
 
         def body(t, carry):
-            base = (step * block + t) * fanout
+            base = step * block + t
             acc = table_ref[pl.ds(index_ref[base], 1), :]
             for k in range(1, fanout):
-                acc = acc + table_ref[pl.ds(index_ref[base + k], 1), :]
+                acc = acc + table_ref[pl.ds(index_ref[k * count + base], 1), :]
             out_ref[pl.ds(t, 1), :] = acc
             return carry
 
@@ -58,11 +58,10 @@
     hidden_width = self_first.shape[1]
     feat_size = lax.axis_size("feat")
     share_rows = targets_part // feat_size
-    node_rows = features.T
     mixed_rows = (
-        gather_sum(node_rows.astype(jnp.float32), neighbours) / fanout_first
+        gather_sum(features.astype(jnp.float32).T, neighbours.T) / fanout_first
     ).astype(jnp.bfloat16)
-    own_rows = node_rows[:targets_part]
+    own_rows = features[:, :targets_part].T
     both = jnp.stack([own_rows, mixed_rows], axis=1).reshape(
         feat_size, share_rows, 2, columns_here
     )
@@ -86,6 +85,7 @@
         (flat_rows[:, k : k + 1] == table_index).astype(jnp.bfloat16)
         for k in range(fanout_second)
     )
+    counts = lax.optimization_barrier(counts)
     summed = jnp.dot(counts, segment, preferred_element_type=jnp.float32)
     mean_second = (summed / fanout_second).astype(jnp.bfloat16)
     second_out = (

time: 454 us -> 419 us (0.923)
  waiting for transfers between devices: 261 us -> 239 us
  other arithmetic: 9.53 us -> 28.4 us
  matrix products: 46.5 us -> 27.7 us
  local copies, waits for them, and re-layouts: 27.7 us -> 20.2 us
    add x0 -> x1, other arithmetic: none -> 24.9 us  [shards(): sum(((flat_rows[:, k:k + 1] == table_index).astype(jnp.bfloat16) for k in...]
    all_gather x1, waiting for transfers between devices: 104 us -> 81.7 us  [shards(): segment = lax.all_gather(layer_out, 'dom', axis=0, tiled=True)]
    dot_general x1, matrix products: 32.4 us -> 14.9 us  [shards(): summed = jnp.dot(counts, segment, preferred_element_type=jnp.float32)]
    unnamed x27 -> x30, local copies, waits for them, and re-layouts: 18.3 us -> 9.02 us
    transpose x0 -> x1, local copies, waits for them, and re-layouts: none -> 6.44 us  [shards(): features.astype(jnp.float32)]
    convert_element_type x2 -> x1, other arithmetic: 6.83 us -> 1.75 us  [shards(): mixed_rows = (gather_sum(features.astype(jnp.float32).T, neighbours.T) /...]
  transfers between devices with their start and end apart: 2 -> 2, of which waited for: 2 -> 2; matrix products, arithmetic and copies ran while one was open for 3% -> 8% of each run, Pallas kernels for 0% -> 0%
where the time goes in v3:
time: 419 us
  waiting for transfers between devices  239 us (57%)
  Pallas kernels  62.6 us (15%)
  other arithmetic  28.4 us (7%)
  matrix products  27.7 us (7%)
  blocking collectives  26.3 us (6%)
  local copies, waits for them, and re-layouts  20.2 us (5%)
  between operations  14.2 us (3%)
    psum x1, waiting for transfers between devices, shards(): lax.psum((grad_self, grad_neighbour), ('feat', 'dom'))  157 us
    all_gather x1, waiting for transfers between devices, shards(): segment = lax.all_gather(layer_out, 'dom', axis=0, tiled=True)  81.7 us
    pallas_call x1, Pallas kernels, gather_sum(): pl.pallas_call(kernel, out_shape=jax.ShapeDtypeStruct((count, width), jnp...  62.6 us
    all_to_all x1, blocking collectives, shards(): arrived = lax.all_to_all(both, 'feat', 0, 0, tiled=True)  26.3 us
    add x1, other arithmetic, shards(): sum(((flat_rows[:, k:k + 1] == table_index).astype(jnp.bfloat16) for k in...  24.9 us
    dot_general x1, matrix products, shards(): summed = jnp.dot(counts, segment, preferred_element_type=jnp.float32)  14.9 us
    unnamed x30, local copies, waits for them, and re-layouts  9.02 us
  transfers between devices with their start and end apart: 2, of which 2 were waited for; matrix products, arithmetic and copies ran while one was open for 8% of the time, Pallas kernels for 0%

profile of v3, /device:TPU:1, one launch (start us, length us, event | category | flops | bytes accessed | tf_op | source)
XLA Modules:
  0.0 418.5 jit_solution(12432876604061682866)
XLA Ops:
  7.2 0.0 copy-start
  7.2 0.0 all-gather.2.cloned.1.call-start
  7.2 0.0 copy-start.7
  7.2 0.0 slice-start
  7.2 6.4 %copy.22 = f32[96,16384]{0,1:T(8,128)} copy(bf16[96,16384]{1,0:T(8,128)(2,1)} %param.9) | data formatting | bytes 9437184 | tf_op jit(solution)/shard_map/transpose | solution.py:62
  13.7 0.0 copy-done.7
  13.7 0.8 reshape.19.index_ref
  14.5 0.0 slice-done
  14.5 0.3 copy.27
  14.7 1.1 copy.23
  15.9 62.6 %shard_map.112 = f32[4096,96]{1,0:T(8,128)} custom-call(s32[61440]{0:T(1024)} %reshape.19.index_ref, f32[16384,96]{1,0:T(8,128)} %bitcast.30), custom_call_target="tpu_custom_call" | custom-call | tf_op jit(solution)/shard_map/pallas_call | solution.py:32
  78.5 1.8 multiply_convert_fusion.1
  80.2 1.2 copy.24
  81.5 0.0 copy-start.11
  81.5 0.0 copy-start.12
  81.5 1.7 pad_maximum_fusion
  83.1 26.3 %all_to_all.5 = bf16[8,512,2,96]{1,3,2,0:T(8,128)(2,1)S(1)} all-to-all(bf16[8,512,2,96]{1,3,2,0:T(8,128)(2,1)S(1)} %pad_maximum_fusion), channel_id=1, replica_groups=mesh['feat'=8,'dom'=16] {'feat'}, dimensions={0} | all-to-all | bytes 3145728 | tf_op jit(solution)/shard_map/all_to_all | solution.py:68
  109.5 0.0 copy-done.11
  109.5 0.0 copy-done.12
  109.5 0.0 copy-start.9
  109.5 0.0 copy-start.8
  109.5 2.8 fusion.23
  112.3 0.0 all-gather.2.cloned.1.call-update
  112.3 0.2 all-reduce.3.cloned.1.call-start
  112.5 0.0 copy-done.9
  112.5 0.1 multiply_reduce_fusion
  112.6 0.2 mul.11
  112.8 0.0 copy-done.8
  112.8 0.1 copy.25
  113.0 1.4 slice_reduce_fusion.9
  114.4 0.0 copy-start.1
  114.4 0.0 copy-start.3
  114.4 24.9 %fusion.10 = bf16[512,8192]{1,0:T(8,128)(2,1)} fusion(s32[512]{0:T(512)S(1)} %get-tuple-element.4, s32[512]{0:T(512)S(1)} %get-tuple-element.5, s32[512]{0:T(512)S(1)} %get-tuple-element.6, s32[512]{0:T(512)S(1)} %get-tuple-element.7, s32[512]{0:T(512)S(1)} %get-tuple-element.8, s32[512]{0:T(512)S(1)} %get-tuple-element.9, s32[512]{0:T(512)S(1)} %get-tuple-element.10, ...), kind=kLoop, calls=%fused_computation.20 | loop fusion | flops 167772160 | bytes 8409088 | tf_op jit(solution)/shard_map/add | solution.py:84
  139.3 0.0 copy-done.1
  139.3 0.0 copy-done.3
  139.3 3.3 fusion.29
  142.7 81.7 %all-gather.2.cloned.1.call-done = bf16[8192,1024]{1,0:T(8,128)(2,1)} async-done(((bf16[512,1024]{1,0:T(8,128)(2,1)}), bf16[8192,1024]{1,0:T(8,128)(2,1)}) %all-gather.2.cloned.1.call-update) | async-done | bytes 16777232 | tf_op jit(solution)/shard_map/all_gather | solution.py:81
  224.3 0.0 copy-start.4
  224.3 14.9 %multiply_convert_fusion = bf16[512,1024]{1,0:T(8,128)(2,1)S(1)} fusion(bf16[512,8192]{1,0:T(8,128)(2,1)} %fusion.10, bf16[8192,1024]{1,0:T(8,128)(2,1)} %all-gather.2.cloned.1.call-done), kind=kOutput, calls=%fused_computation.36 | convolution fusion | flops 8590983168 | bytes 26214400 | tf_op jit(solution)/shard_map/dot_general | solution.py:89
  239.2 0.0 copy-start.5
  239.2 1.0 copy-done.5
  240.2 0.0 copy-done.4
  240.2 3.3 fusion.30
  243.5 0.0 all-reduce.3.cloned.1.call-update
  243.5 0.0 copy-done
  243.5 0.0 copy-start.6
  243.5 0.0 copy-start.10
  243.5 1.3 fusion.28
  244.8 0.0 copy-done.6
  244.8 0.6 copy-done.10
  245.4 2.2 add_convert_fusion
  247.7 157.1 %all-reduce.3.cloned.1.call-done = (f32[1024,1024]{1,0:T(8,128)}, f32[1024,1024]{1,0:T(8,128)}) async-done(((f32[1024,1024]{1,0:T(8,128)}, f32[1024,1024]{1,0:T(8,128)}), (f32[1024,1024]{1,0:T(8,128)}, f32[1024,1024]{1,0:T(8,128)})) %all-reduce.3.cloned.1.call-update) | async-done | bytes 8388624 | tf_op jit(solution)/shard_map/psum | solution.py:97
  404.8 0.0 copy-start.2
  404.8 4.9 %copy.30 = f32[1024,1024]{1,0:T(8,128)} copy(f32[1024,1024]{1,0:T(8,128)} %get-tuple-element.16) | data formatting | bytes 8388608
  409.7 0.0 copy-done.2
  409.7 2.0 copy.31
  (1 shorter events, 0.0 us)
Async XLA Ops:
  7.2 236.3 %copy-start = (bf16[1024,1024]{1,0:T(8,128)(2,1)S(1)}, bf16[1024,1024]{1,0:T(8,128)(2,1)}, u32[]{:S(2)}) copy-start(bf16[1024,1024]{1,0:T(8,128)(2,1)} %param.15) | copy-start | bytes 6291460
  7.2 217.2 %all-gather.2.cloned.1.call-start = ((), (), s32[]{:S(2)}) async-start(), calls=%async_computation.1 | async-start | bytes 17825792 | tf_op jit(solution)/shard_map/all_gather | solution.py:81
  7.2 6.5 %copy-start.7 = (s32[4096,15]{0,1:T(8,128)S(1)}, s32[4096,15]{0,1:T(8,128)}, u32[]{:S(2)}) copy-start(s32[4096,15]{0,1:T(8,128)} %param.10) | copy-start | bytes 737284
  7.2 7.2 %slice-start = ((bf16[96,16384]{1,0:T(8,128)(2,1)}), bf16[96,4096]{1,0:T(8,128)(2,1)S(1)}, s32[]{:S(2)}) async-start(bf16[96,16384]{1,0:T(8,128)(2,1)} %param.9), calls=%async_computation.3 | async-start | bytes 1572864 | tf_op jit(solution)/shard_map/slice | solution.py:64
  81.5 28.0 %copy-start.11 = (bf16[768,1024]{1,0:T(8,128)(2,1)S(1)}, bf16[768,1024]{1,0:T(8,128)(2,1)}, u32[]{:S(2)}) copy-start(bf16[768,1024]{1,0:T(8,128)(2,1)} %param.12) | copy-start | bytes 4718596
  81.5 28.0 %copy-start.12 = (bf16[768,1024]{1,0:T(8,128)(2,1)S(1)}, bf16[768,1024]{1,0:T(8,128)(2,1)}, u32[]{:S(2)}) copy-start(bf16[768,1024]{1,0:T(8,128)(2,1)} %param.11) | copy-start | bytes 4718596
  109.5 3.1 copy-start.9
  109.5 3.4 copy-start.8
  112.3 292.5 %all-reduce.3.cloned.1.call-start = ((), (), s32[]{:S(2)}) async-start(), calls=%async_computation.2 | async-start | bytes 16777216 | tf_op jit(solution)/shard_map/psum | solution.py:97
  114.4 24.9 %copy-start.1 = (bf16[512,1024]{1,0:T(8,128)(2,1)S(1)}, bf16[512,1024]{1,0:T(8,128)(2,1)}, u32[]{:S(2)}) copy-start(bf16[512,1024]{1,0:T(8,128)(2,1)} %fusion.23) | copy-start | bytes 3145732
  114.4 24.9 %copy-start.3 = (bf16[512,1024]{1,0:T(8,128)(2,1)S(1)}, bf16[512,1024]{1,0:T(8,128)(2,1)}, u32[]{:S(2)}) copy-start(bf16[512,1024]{1,0:T(8,128)(2,1)} %param.17) | copy-start | bytes 3145732
  224.3 15.8 %copy-start.4 = (bf16[512,1024]{1,0:T(8,128)(2,1)S(1)}, bf16[512,1024]{1,0:T(8,128)(2,1)}, u32[]{:S(2)}) copy-start(bf16[512,1024]{1,0:T(8,128)(2,1)} %param.17) | copy-start | bytes 3145732
  239.2 1.0 copy-start.5
  243.5 1.3 copy-start.6
  243.5 1.9 copy-start.10
  404.8 4.9 %copy-start.2 = (f32[1024,1024]{1,0:T(8,128)S(1)}, f32[1024,1024]{1,0:T(8,128)}, u32[]{:S(2)}) copy-start(f32[1024,1024]{1,0:T(8,128)} %get-tuple-element.17) | copy-start | bytes 12582916
Sparse Core Ops, SparseCore 0:
  112.4 111.8 all-gather.1
  243.6 161.0 all-reduce.2

commit v4 on v3

--- a/solution.py
+++ b/solution.py
@@ -58,15 +58,8 @@
     hidden_width = self_first.shape[1]
     feat_size = lax.axis_size("feat")
     share_rows = targets_part // feat_size
-    mixed_rows = (
-        gather_sum(features.astype(jnp.float32).T, neighbours.T) / fanout_first
-    ).astype(jnp.bfloat16)
-    own_rows = features[:, :targets_part].T
-    both = jnp.stack([own_rows, mixed_rows], axis=1).reshape(
-        feat_size, share_rows, 2, columns_here
-    )
-    arrived = lax.all_to_all(both, "feat", 0, 0, tiled=True)
-    lhs = jnp.transpose(arrived, (1, 0, 2, 3)).reshape(share_rows, -1)
+    pieces = 2
+    piece_rows = share_rows // pieces
     weights = jnp.stack(
         [
             self_first.reshape(feat_size, columns_here, hidden_width),
@@ -74,19 +67,40 @@
         ],
         axis=1,
     ).reshape(-1, hidden_width)
-    pre_first = jnp.dot(lhs, weights, preferred_element_type=jnp.float32)
-    layer_out = jnp.maximum(pre_first, 0.0).astype(jnp.bfloat16)
+    table = features.astype(jnp.float32).T
+    lists = neighbours.T.reshape(fanout_first, feat_size, share_rows)
+    own_all = features[:, :targets_part].reshape(columns_here, feat_size, share_rows)
     seed_rows = cotangent.shape[0]
     fanout_second = offsets.shape[1]
-    segment = lax.all_gather(layer_out, "dom", axis=0, tiled=True)
-    flat_rows = owners.reshape(seed_rows, fanout_second) * share_rows + offsets
-    table_index = jnp.arange(segment.shape[0], dtype=jnp.int32)[None, :]
-    counts = sum(
-        (flat_rows[:, k : k + 1] == table_index).astype(jnp.bfloat16)
-        for k in range(fanout_second)
-    )
-    counts = lax.optimization_barrier(counts)
-    summed = jnp.dot(counts, segment, preferred_element_type=jnp.float32)
+    slot_owner = owners.reshape(seed_rows, fanout_second)
+    layer_parts = []
+    summed = None
+    for c in range(pieces):
+        rows = slice(c * piece_rows, (c + 1) * piece_rows)
+        mixed_rows = (
+            gather_sum(table, lists[:, :, rows].reshape(fanout_first, -1)) / fanout_first
+        ).astype(jnp.bfloat16)
+        own_rows = jnp.transpose(own_all[:, :, rows], (1, 2, 0))
+        both = jnp.stack(
+            [own_rows, mixed_rows.reshape(feat_size, piece_rows, columns_here)], axis=2
+        )
+        arrived = lax.all_to_all(both, "feat", 0, 0, tiled=True)
+        lhs = jnp.transpose(arrived, (1, 0, 2, 3)).reshape(piece_rows, -1)
+        pre_first = jnp.dot(lhs, weights, preferred_element_type=jnp.float32)
+        part_out = jnp.maximum(pre_first, 0.0).astype(jnp.bfloat16)
+        layer_parts.append(part_out)
+        segment = lax.all_gather(part_out, "dom", axis=0, tiled=True)
+        inside = offsets // piece_rows == c
+        flat_rows = jnp.where(inside, slot_owner * piece_rows + offsets - c * piece_rows, -1)
+        table_index = jnp.arange(segment.shape[0], dtype=jnp.int32)[None, :]
+        counts = sum(
+            (flat_rows[:, k : k + 1] == table_index).astype(jnp.bfloat16)
+            for k in range(fanout_second)
+        )
+        counts = lax.optimization_barrier(counts)
+        term = jnp.dot(counts, segment, preferred_element_type=jnp.float32)
+        summed = term if summed is None else summed + term
+    layer_out = jnp.concatenate(layer_parts, axis=0)
     mean_second = (summed / fanout_second).astype(jnp.bfloat16)
     second_out = (
         jnp.dot(layer_out, self_second, preferred_element_type=jnp.float32)

time: 419 us -> 407 us (0.971)
  waiting for transfers between devices: 239 us -> 201 us
  matrix products: 27.7 us -> 39.3 us
  blocking collectives: 26.3 us -> 33.3 us
  Pallas kernels: 62.6 us -> 67.4 us
    all_gather x1 -> x2, waiting for transfers between devices: 81.7 us -> 44.6 us  [shards(): segment = lax.all_gather(part_out, 'dom', axis=0, tiled=True)]
    all_to_all x1 -> x2, blocking collectives: 26.3 us -> 33.3 us  [shards(): arrived = lax.all_to_all(both, 'feat', 0, 0, tiled=True)]
    dot_general x1 -> x2, matrix products: 14.9 us -> 20.4 us  [shards(): term = jnp.dot(counts, segment, preferred_element_type=jnp.float32)]
    dot_general x1 -> x2, matrix products: 2.79 us -> 7.53 us  [shards(): pre_first = jnp.dot(lhs, weights, preferred_element_type=jnp.float32)]
    pallas_call x1 -> x2, Pallas kernels: 62.6 us -> 67.4 us  [gather_sum(): pl.pallas_call(kernel, out_shape=jax.ShapeDtypeStruct((count, width), jnp...]
    add x1 -> x2, other arithmetic: 24.9 us -> 27 us  [shards(): sum(((flat_rows[:, k:k + 1] == table_index).astype(jnp.bfloat16) for k in...]
  transfers between devices with their start and end apart: 2 -> 3, of which waited for: 2 -> 2; matrix products, arithmetic and copies ran while one was open for 8% -> 14% of each run, Pallas kernels for 0% -> 8%
where the time goes in v4:
time: 407 us; the launch traced here: 406 us
  waiting for transfers between devices  201 us (49%)
  Pallas kernels  67.4 us (17%)
  matrix products  39.3 us (10%)
  blocking collectives  33.3 us (8%)
  other arithmetic  30.3 us (7%)
  local copies, waits for them, and re-layouts  20.9 us (5%)
  between operations  14 us (3%)
    psum x1, waiting for transfers between devices, shards(): lax.psum((grad_self, grad_neighbour), ('feat', 'dom'))  156 us
    pallas_call x2, Pallas kernels, gather_sum(): pl.pallas_call(kernel, out_shape=jax.ShapeDtypeStruct((count, width), jnp...  67.4 us
    all_gather x2, waiting for transfers between devices, shards(): segment = lax.all_gather(part_out, 'dom', axis=0, tiled=True)  44.6 us
    all_to_all x2, blocking collectives, shards(): arrived = lax.all_to_all(both, 'feat', 0, 0, tiled=True)  33.3 us
    add x2, other arithmetic, shards(): sum(((flat_rows[:, k:k + 1] == table_index).astype(jnp.bfloat16) for k in...  27 us
    dot_general x2, matrix products, shards(): term = jnp.dot(counts, segment, preferred_element_type=jnp.float32)  20.4 us
    unnamed x30, local copies, waits for them, and re-layouts  10.2 us
  transfers between devices with their start and end apart: 3, of which 2 were waited for; matrix products, arithmetic and copies ran while one was open for 14% of the time, Pallas kernels for 8%

profile of v4, /device:TPU:1, one launch (start us, length us, event | category | flops | bytes accessed | tf_op | source)
XLA Modules:
  0.0 406.5 jit_solution(6538257656232161168)
XLA Ops:
  7.2 0.0 copy-start
  7.2 0.0 slice-start
  7.2 0.0 copy-start.6
  7.2 0.0 all-gather.3.cloned.1.call-start
  7.2 6.5 %copy.37 = f32[96,16384]{0,1:T(8,128)} copy(bf16[96,16384]{1,0:T(8,128)(2,1)} %param.9) | data formatting | bytes 9437184 | tf_op jit(solution)/shard_map/transpose | solution.py:70
  13.7 0.0 copy-done.6
  13.7 0.2 copy.51
  13.9 0.0 slice-done
  13.9 0.3 copy.50
  14.2 0.8 fusion.56
  15.0 0.7 copy.52
  15.7 33.7 %shard_map.112 = f32[2048,96]{1,0:T(8,128)} custom-call(s32[30720]{0:T(1024)} %bitcast.69, f32[16384,96]{1,0:T(8,128)} %bitcast.59), custom_call_target="tpu_custom_call" | custom-call | tf_op jit(solution)/shard_map/pallas_call | solution.py:32
  49.4 1.3 multiply_convert_fusion.2
  50.7 0.2 copy.38
  50.9 1.1 copy.57
  52.0 0.1 pad_maximum_fusion.16
  52.1 17.9 %all_to_all.10 = bf16[8,256,2,96]{1,3,2,0:T(8,128)(2,1)S(1)} all-to-all(bf16[8,256,2,96]{1,3,2,0:T(8,128)(2,1)S(1)} %pad_maximum_fusion.16), channel_id=1, replica_groups=mesh['feat'=8,'dom'=16] {'feat'}, dimensions={0} | all-to-all | bytes 1572864 | tf_op jit(solution)/shard_map/all_to_all | solution.py:87
  70.0 3.7 fusion.44
  73.7 0.0 all-gather.3.cloned.1.call-update
  73.7 0.0 all-gather.5.cloned.1.call-start
  73.8 0.7 copy.53
  74.5 33.7 %shard_map.113 = f32[2048,96]{1,0:T(8,128)} custom-call(s32[30720]{0:T(1024)} %bitcast.68, f32[16384,96]{1,0:T(8,128)} %bitcast.60), custom_call_target="tpu_custom_call" | custom-call | tf_op jit(solution)/shard_map/pallas_call | solution.py:32
  108.1 1.6 multiply_convert_fusion.1
  109.8 0.2 copy.40
  110.0 0.1 copy.56
  110.1 0.1 pad_maximum_fusion.17
  110.1 15.4 %all_to_all.11 = bf16[8,256,2,96]{1,3,2,0:T(8,128)(2,1)S(1)} all-to-all(bf16[8,256,2,96]{1,3,2,0:T(8,128)(2,1)S(1)} %pad_maximum_fusion.17), channel_id=1, replica_groups=mesh['feat'=8,'dom'=16] {'feat'}, dimensions={0} | all-to-all | bytes 1572864 | tf_op jit(solution)/shard_map/all_to_all | solution.py:87
  125.6 0.0 copy-start.8
  125.6 0.0 copy-start.7
  125.6 3.8 fusion.45
  129.4 0.0 all-gather.5.cloned.1.call-update
  129.5 0.2 all-reduce.3.cloned.1.call-start
  129.7 0.0 copy-done.8
  129.7 0.1 multiply_reduce_fusion
  129.8 0.2 mul.8
  130.0 0.0 copy-done.7
  130.0 0.1 copy.41
  130.1 0.2 add_select_fusion.1
  130.3 1.4 slice_reduce_fusion.19
  131.7 13.5 %fusion.29 = bf16[512,4096]{1,0:T(8,128)(2,1)} fusion(s32[512]{0:T(512)S(1)} %get-tuple-element.14, s32[512]{0:T(512)S(1)} %get-tuple-element.15, s32[512]{0:T(512)S(1)} %get-tuple-element.16, s32[512]{0:T(512)S(1)} %get-tuple-element.17, s32[512]{0:T(512)S(1)} %get-tuple-element.18, s32[512]{0:T(512)S(1)} %get-tuple-element.19, ...), kind=kLoop, calls=%fused_computation.49 | loop fusion | flops 83886080 | bytes 4214784 | tf_op jit(solution)/shard_map/add | solution.py:96
  145.2 0.0 copy-start.2
  145.2 0.0 copy-start.4
  145.2 0.0 copy-start.5
  145.2 1.4 slice_reduce_fusion.9
  146.6 13.5 %fusion.20 = bf16[512,4096]{1,0:T(8,128)(2,1)} fusion(s32[512]{0:T(512)S(1)} %get-tuple-element.4, s32[512]{0:T(512)S(1)} %get-tuple-element.5, s32[512]{0:T(512)S(1)} %get-tuple-element.6, s32[512]{0:T(512)S(1)} %get-tuple-element.7, s32[512]{0:T(512)S(1)} %get-tuple-element.8, s32[512]{0:T(512)S(1)} %get-tuple-element.9, s32[512]{0:T(512)S(1)} %get-tuple-element.10, ...), kind=kLoop, calls=%fused_computation.40 | loop fusion | flops 83886080 | bytes 4214784 | tf_op jit(solution)/shard_map/add | solution.py:96
  160.1 0.0 copy-done.2
  160.1 0.0 copy-done.4
  160.1 0.0 copy-done.5
  160.1 3.2 fusion.48
  163.3 10.7 %fusion.57 = f32[512,1024]{1,0:T(8,128)} fusion(bf16[512,4096]{1,0:T(8,128)(2,1)} %fusion.29, bf16[4096,1024]{1,0:T(8,128)(2,1)} %all-gather.3.cloned.1.call-done), kind=kOutput, calls=%fused_computation.117 | convolution fusion | flops 4294967296 | bytes 14680064 | tf_op jit(solution)/shard_map/dot_general | solution.py:101
  174.0 44.6 %all-gather.5.cloned.1.call-done = bf16[4096,1024]{1,0:T(8,128)(2,1)} async-done(((bf16[256,1024]{1,0:T(8,128)(2,1)}), bf16[4096,1024]{1,0:T(8,128)(2,1)}) %all-gather.5.cloned.1.call-update) | async-done | bytes 8388624 | tf_op jit(solution)/shard_map/all_gather | solution.py:92
  218.6 9.7 %multiply_convert_fusion = bf16[512,1024]{1,0:T(8,128)(2,1)S(1)} fusion(f32[512,1024]{1,0:T(8,128)} %fusion.57, bf16[512,4096]{1,0:T(8,128)(2,1)} %fusion.20, bf16[4096,1024]{1,0:T(8,128)(2,1)} %all-gather.5.cloned.1.call-done), kind=kOutput, calls=%fused_computation.60 | convolution fusion | flops 4296540160 | bytes 15728640 | tf_op jit(solution)/shard_map/dot_general | solution.py:101
  228.4 0.0 copy-done.3
  228.4 3.3 fusion.58
  231.7 0.0 all-reduce.3.cloned.1.call-update
  231.7 0.0 copy-done
  231.7 0.0 copy-start.9
  231.7 2.6 fusion.49
  234.3 0.0 copy-done.9
  234.4 2.3 add_convert_fusion
  236.6 156.4 %all-reduce.3.cloned.1.call-done = (f32[1024,1024]{1,0:T(8,128)}, f32[1024,1024]{1,0:T(8,128)}) async-done(((f32[1024,1024]{1,0:T(8,128)}, f32[1024,1024]{1,0:T(8,128)}), (f32[1024,1024]{1,0:T(8,128)}, f32[1024,1024]{1,0:T(8,128)})) %all-reduce.3.cloned.1.call-update) | async-done | bytes 8388624 | tf_op jit(solution)/shard_map/psum | solution.py:111
  393.0 4.9 %copy.60 = f32[1024,1024]{1,0:T(8,128)} copy(f32[1024,1024]{1,0:T(8,128)} %get-tuple-element.32) | data formatting | bytes 8388608
  397.9 0.0 copy-done.1
  397.9 2.0 copy.61
  (5 shorter events, 0.0 us)
Async XLA Ops:
  7.2 224.6 %copy-start = (bf16[1024,1024]{1,0:T(8,128)(2,1)S(1)}, bf16[1024,1024]{1,0:T(8,128)(2,1)}, u32[]{:S(2)}) copy-start(bf16[1024,1024]{1,0:T(8,128)(2,1)} %param.15) | copy-start | bytes 6291460
  7.2 6.8 %slice-start = ((bf16[96,16384]{1,0:T(8,128)(2,1)}), bf16[96,4096]{1,0:T(8,128)(2,1)S(1)}, s32[]{:S(2)}) async-start(bf16[96,16384]{1,0:T(8,128)(2,1)} %param.9), calls=%async_computation.5 | async-start | bytes 1572864 | tf_op jit(solution)/shard_map/slice | solution.py:72
  7.2 6.5 %copy-start.6 = (s32[4096,15]{0,1:T(8,128)S(1)}, s32[4096,15]{0,1:T(8,128)}, u32[]{:S(2)}) copy-start(s32[4096,15]{0,1:T(8,128)} %param.10) | copy-start | bytes 737284
  7.2 156.1 %all-gather.3.cloned.1.call-start = ((), (), s32[]{:S(2)}) async-start(), calls=%async_computation.2 | async-start | bytes 8912896 | tf_op jit(solution)/shard_map/all_gather | solution.py:92
  73.7 144.9 %all-gather.5.cloned.1.call-start = ((), (), s32[]{:S(2)}) async-start(), calls=%async_computation.3 | async-start | bytes 8912896 | tf_op jit(solution)/shard_map/all_gather | solution.py:92
  125.6 4.1 %copy-start.8 = (s32[5120,1]{0,1:T(1,128)S(1)}, s32[5120,1]{0,1:T(1,128)}, u32[]{:S(2)}) copy-start(s32[5120,1]{0,1:T(1,128)} %param.13) | copy-start | bytes 61444
  125.6 4.4 %copy-start.7 = (s32[512,10]{0,1:T(8,128)S(1)}, s32[512,10]{0,1:T(8,128)}, u32[]{:S(2)}) copy-start(s32[512,10]{0,1:T(8,128)} %param.14) | copy-start | bytes 61444
  129.5 263.5 %all-reduce.3.cloned.1.call-start = ((), (), s32[]{:S(2)}) async-start(), calls=%async_computation.4 | async-start | bytes 16777216 | tf_op jit(solution)/shard_map/psum | solution.py:111
  145.2 14.9 %copy-start.2 = (bf16[512,1024]{1,0:T(8,128)(2,1)S(1)}, bf16[512,1024]{1,0:T(8,128)(2,1)}, u32[]{:S(2)}) copy-start(bf16[512,1024]{1,0:T(8,128)(2,1)} %param.17) | copy-start | bytes 3145732
  145.2 14.9 %copy-start.4 = (bf16[256,1024]{1,0:T(8,128)(2,1)S(1)}, bf16[256,1024]{1,0:T(8,128)(2,1)}, u32[]{:S(2)}) copy-start(bf16[256,1024]{1,0:T(8,128)(2,1)} %fusion.44) | copy-start | bytes 1572868
  145.2 14.9 %copy-start.5 = (bf16[256,1024]{1,0:T(8,128)(2,1)S(1)}, bf16[256,1024]{1,0:T(8,128)(2,1)}, u32[]{:S(2)}) copy-start(bf16[256,1024]{1,0:T(8,128)(2,1)} %fusion.45) | copy-start | bytes 1572868
  218.6 9.8 %copy-start.3 = (bf16[512,1024]{1,0:T(8,128)(2,1)S(1)}, bf16[512,1024]{1,0:T(8,128)(2,1)}, u32[]{:S(2)}) copy-start(bf16[512,1024]{1,0:T(8,128)(2,1)} %param.17) | copy-start | bytes 3145732
  231.7 2.6 copy-start.9
  393.0 4.9 %copy-start.1 = (f32[1024,1024]{1,0:T(8,128)S(1)}, f32[1024,1024]{1,0:T(8,128)}, u32[]{:S(2)}) copy-start(f32[1024,1024]{1,0:T(8,128)} %get-tuple-element.33) | copy-start | bytes 12582916
Sparse Core Ops, SparseCore 0:
  73.8 71.4 all-gather.2
  148.1 70.5 all-gather.4
  231.8 161.1 all-reduce.2

commit v5 on v4

--- a/solution.py
+++ b/solution.py
@@ -58,8 +58,7 @@
     hidden_width = self_first.shape[1]
     feat_size = lax.axis_size("feat")
     share_rows = targets_part // feat_size
-    pieces = 2
-    piece_rows = share_rows // pieces
+    cuts = [0, 3 * share_rows // 8, share_rows]
     weights = jnp.stack(
         [
             self_first.reshape(feat_size, columns_here, hidden_width),
@@ -75,8 +74,9 @@
     slot_owner = owners.reshape(seed_rows, fanout_second)
     layer_parts = []
     summed = None
-    for c in range(pieces):
-        rows = slice(c * piece_rows, (c + 1) * piece_rows)
+    for c in range(len(cuts) - 1):
+        first, piece_rows = cuts[c], cuts[c + 1] - cuts[c]
+        rows = slice(first, first + piece_rows)
         mixed_rows = (
             gather_sum(table, lists[:, :, rows].reshape(fanout_first, -1)) / fanout_first
         ).astype(jnp.bfloat16)
@@ -90,8 +90,8 @@
         part_out = jnp.maximum(pre_first, 0.0).astype(jnp.bfloat16)
         layer_parts.append(part_out)
         segment = lax.all_gather(part_out, "dom", axis=0, tiled=True)
-        inside = offsets // piece_rows == c
-        flat_rows = jnp.where(inside, slot_owner * piece_rows + offsets - c * piece_rows, -1)
+        inside = (offsets >= first) & (offsets < first + piece_rows)
+        flat_rows = jnp.where(inside, slot_owner * piece_rows + offsets - first, -1)
         table_index = jnp.arange(segment.shape[0], dtype=jnp.int32)[None, :]
         counts = sum(
             (flat_rows[:, k : k + 1] == table_index).astype(jnp.bfloat16)

time: 407 us -> 407 us (level)
  blocking collectives: 33.3 us -> 38.9 us
    all_to_all x2, blocking collectives: 33.3 us -> 38.9 us  [shards(): arrived = lax.all_to_all(both, 'feat', 0, 0, tiled=True)]
    unnamed x30 -> x25, local copies, waits for them, and re-layouts: 10.2 us -> 7.16 us
  transfers between devices with their start and end apart: 3 -> 3, of which waited for: 2 -> 2; matrix products, arithmetic and copies ran while one was open for 14% -> 13% of each run, Pallas kernels for 8% -> 10%
where the time goes in v5:
time: 407 us; the launch traced here: 406 us
  waiting for transfers between devices  198 us (49%)
  Pallas kernels  67.6 us (17%)
  blocking collectives  38.9 us (10%)
  matrix products  37.8 us (9%)
  other arithmetic  30.3 us (7%)
  local copies, waits for them, and re-layouts  19.8 us (5%)
  between operations  14 us (3%)
    psum x1, waiting for transfers between devices, shards(): lax.psum((grad_self, grad_neighbour), ('feat', 'dom'))  157 us
    pallas_call x2, Pallas kernels, gather_sum(): pl.pallas_call(kernel, out_shape=jax.ShapeDtypeStruct((count, width), jnp...  67.6 us
    all_gather x2, waiting for transfers between devices, shards(): segment = lax.all_gather(part_out, 'dom', axis=0, tiled=True)  41.2 us
    all_to_all x2, blocking collectives, shards(): arrived = lax.all_to_all(both, 'feat', 0, 0, tiled=True)  38.9 us
    add x2, other arithmetic, shards(): sum(((flat_rows[:, k:k + 1] == table_index).astype(jnp.bfloat16) for k in...  27.1 us
    dot_general x2, matrix products, shards(): term = jnp.dot(counts, segment, preferred_element_type=jnp.float32)  18.9 us
  transfers between devices with their start and end apart: 3, of which 2 were waited for; matrix products, arithmetic and copies ran while one was open for 13% of the time, Pallas kernels for 10%

profile of v5, /device:TPU:1, one launch (start us, length us, event | category | flops | bytes accessed | tf_op | source)
XLA Modules:
  0.0 406.3 jit_solution(6615293669124846752)
XLA Ops:
  7.2 0.0 copy-start
  7.2 0.0 copy-start.7
  7.2 0.0 all-gather.3.cloned.1.call-start
  7.2 6.5 %copy.59 = f32[96,16384]{0,1:T(8,128)} copy(bf16[96,16384]{1,0:T(8,128)(2,1)} %param.9) | data formatting | bytes 9437184 | tf_op jit(solution)/shard_map/transpose | solution.py:69
  13.7 0.0 copy-done.7
  13.7 0.2 copy.66
  13.9 0.7 reshape_reshape.6.index_ref
  14.7 0.0 slice-start
  14.7 26.6 %shard_map.112 = f32[1536,96]{1,0:T(8,128)} custom-call(s32[23040]{0:T(1024)} %reshape_reshape.6.index_ref, f32[16384,96]{1,0:T(8,128)} %bitcast.72), custom_call_target="tpu_custom_call" | custom-call | tf_op jit(solution)/shard_map/pallas_call | solution.py:32
  41.2 1.2 multiply_convert_fusion.2
  42.4 0.0 slice-done
  42.4 1.3 copy.58
  43.7 1.0 slice_bitcast_fusion.1
  44.8 0.2 pad_maximum_fusion.17
  44.9 17.9 %all_to_all.10 = bf16[8,192,2,96]{3,1,2,0:T(8,128)(2,1)S(1)} all-to-all(bf16[8,192,2,96]{3,1,2,0:T(8,128)(2,1)S(1)} %pad_maximum_fusion.17), channel_id=1, replica_groups=mesh['feat'=8,'dom'=16] {'feat'}, dimensions={0} | all-to-all | bytes 1179648 | tf_op jit(solution)/shard_map/all_to_all | solution.py:87
  62.8 3.5 fusion.45
  66.3 0.0 all-gather.3.cloned.1.call-update
  66.3 0.0 all-gather.5.cloned.1.call-start
  66.4 0.1 slice.103
  66.5 0.8 reshape_reshape.7.index_ref
  67.3 0.0 copy-start.1
  67.3 41.0 %shard_map.113 = f32[2560,96]{1,0:T(8,128)} custom-call(s32[38400]{0:T(1024)} %reshape_reshape.7.index_ref, f32[16384,96]{1,0:T(8,128)} %bitcast.73), custom_call_target="tpu_custom_call" | custom-call | tf_op jit(solution)/shard_map/pallas_call | solution.py:32
  108.3 0.0 copy-done.1
  108.4 1.4 multiply_convert_fusion.1
  109.8 0.3 pad_maximum_fusion.9
  110.1 1.5 copy.61
  111.6 21.0 %all_to_all.11 = bf16[8,320,2,96]{1,3,2,0:T(8,128)(2,1)S(1)} all-to-all(bf16[8,320,2,96]{1,3,2,0:T(8,128)(2,1)} %copy.61), channel_id=1, replica_groups=mesh['feat'=8,'dom'=16] {'feat'}, dimensions={0} | all-to-all | bytes 1966080 | tf_op jit(solution)/shard_map/all_to_all | solution.py:87
  132.6 0.0 copy-start.9
  132.6 0.0 copy-start.8
  132.6 4.0 fusion.42
  136.6 0.0 all-gather.5.cloned.1.call-update
  136.6 0.0 all-reduce.3.cloned.1.call-start
  136.6 0.0 copy-done.9
  136.7 0.1 multiply_reduce_fusion
  136.8 0.2 mul.16
  137.0 0.1 copy.62
  137.1 0.2 mul.19
  137.3 0.1 copy.63
  137.4 0.0 copy-done.8
  137.5 0.0 copy-start.3
  137.5 0.0 copy-start.5
  137.5 0.0 copy-start.6
  137.5 10.5 %fusion.29 = bf16[512,3072]{1,0:T(8,128)(2,1)} fusion(s32[512]{0:T(512)S(1)} %bitcast.82, s32[512]{0:T(512)S(1)} %bitcast.83, s32[512]{0:T(512)S(1)} %bitcast.84, s32[512]{0:T(512)S(1)} %bitcast.85, s32[512]{0:T(512)S(1)} %bitcast.86, s32[512]{0:T(512)S(1)} %bitcast.87, s32[512]{0:T(512)S(1)} %bitcast.88, s32[512]{0:T(512)S(1)} %bitcast.89, ...), kind=kLoop, calls=%fused_computation.49 | loop fusion | flops 62914560 | bytes 3166208 | tf_op jit(solution)/shard_map/add | solution.py:96
  148.0 16.6 %fusion.20 = bf16[512,5120]{1,0:T(8,128)(2,1)} fusion(s32[512]{0:T(512)S(1)} %bitcast.92, s32[512]{0:T(512)S(1)} %bitcast.93, s32[512]{0:T(512)S(1)} %bitcast.94, s32[512]{0:T(512)S(1)} %bitcast.95, s32[512]{0:T(512)S(1)} %bitcast.96, s32[512]{0:T(512)S(1)} %bitcast.97, s32[512]{0:T(512)S(1)} %bitcast.98, s32[512]{0:T(512)S(1)} %bitcast.99, ...), kind=kLoop, calls=%fused_computation.40 | loop fusion | flops 104857600 | bytes 5263360 | tf_op jit(solution)/shard_map/add | solution.py:96
  164.7 0.0 copy-done.3
  164.7 0.0 copy-done.5
  164.7 0.0 copy-done.6
  164.7 3.3 fusion.48
  168.0 0.0 all-gather.3.cloned.1.call-done
  168.0 8.5 %fusion.56 = f32[512,1024]{1,0:T(8,128)} fusion(bf16[512,3072]{1,0:T(8,128)(2,1)} %fusion.29, bf16[3072,1024]{1,0:T(8,128)(2,1)} %all-gather.3.cloned.1.call-done), kind=kOutput, calls=%fused_computation.90 | convolution fusion | flops 3221225472 | bytes 11534336 | tf_op jit(solution)/shard_map/dot_general | solution.py:101
  176.5 41.2 %all-gather.5.cloned.1.call-done = bf16[5120,1024]{1,0:T(8,128)(2,1)} async-done(((bf16[320,1024]{1,0:T(8,128)(2,1)}), bf16[5120,1024]{1,0:T(8,128)(2,1)}) %all-gather.5.cloned.1.call-update) | async-done | bytes 10485776 | tf_op jit(solution)/shard_map/all_gather | solution.py:92
  217.7 10.4 %multiply_convert_fusion = bf16[512,1024]{1,0:T(8,128)(2,1)S(1)} fusion(f32[512,1024]{1,0:T(8,128)} %fusion.56, bf16[512,5120]{1,0:T(8,128)(2,1)} %fusion.20, bf16[5120,1024]{1,0:T(8,128)(2,1)} %all-gather.5.cloned.1.call-done), kind=kOutput, calls=%fused_computation.60 | convolution fusion | flops 5370281984 | bytes 18874368 | tf_op jit(solution)/shard_map/dot_general | solution.py:101
  228.1 0.0 copy-done.4
  228.1 3.3 fusion.57
  231.4 0.0 all-reduce.3.cloned.1.call-update
  231.5 0.0 copy-done
  231.5 0.0 copy-start.10
  231.5 2.5 fusion.49
  234.0 0.0 copy-done.10
  234.0 2.3 add_convert_fusion
  236.3 156.5 %all-reduce.3.cloned.1.call-done = (f32[1024,1024]{1,0:T(8,128)}, f32[1024,1024]{1,0:T(8,128)}) async-done(((f32[1024,1024]{1,0:T(8,128)}, f32[1024,1024]{1,0:T(8,128)}), (f32[1024,1024]{1,0:T(8,128)}, f32[1024,1024]{1,0:T(8,128)})) %all-reduce.3.cloned.1.call-update) | async-done | bytes 8388624 | tf_op jit(solution)/shard_map/psum | solution.py:111
  392.8 4.9 %copy.69 = f32[1024,1024]{1,0:T(8,128)} copy(f32[1024,1024]{1,0:T(8,128)} %get-tuple-element.30) | data formatting | bytes 8388608
  397.7 0.0 copy-done.2
  397.7 2.0 copy.70
  (7 shorter events, 0.1 us)
Async XLA Ops:
  7.2 224.3 %copy-start = (bf16[1024,1024]{1,0:T(8,128)(2,1)S(1)}, bf16[1024,1024]{1,0:T(8,128)(2,1)}, u32[]{:S(2)}) copy-start(bf16[1024,1024]{1,0:T(8,128)(2,1)} %param.15) | copy-start | bytes 6291460
  7.2 6.6 %copy-start.7 = (s32[4096,15]{0,1:T(8,128)S(1)}, s32[4096,15]{0,1:T(8,128)}, u32[]{:S(2)}) copy-start(s32[4096,15]{0,1:T(8,128)} %param.10) | copy-start | bytes 737284
  7.2 160.8 %all-gather.3.cloned.1.call-start = ((), (), s32[]{:S(2)}) async-start(), calls=%async_computation.2 | async-start | bytes 6684672 | tf_op jit(solution)/shard_map/all_gather | solution.py:92
  14.7 27.8 %slice-start = ((bf16[96,16384]{1,0:T(8,128)(2,1)}), bf16[96,4096]{1,0:T(8,128)(2,1)S(1)}, s32[]{:S(2)}) async-start(bf16[96,16384]{1,0:T(8,128)(2,1)} %param.9), calls=%async_computation.5 | async-start | bytes 1572864 | tf_op jit(solution)/shard_map/slice | solution.py:71
  66.3 151.3 %all-gather.5.cloned.1.call-start = ((), (), s32[]{:S(2)}) async-start(), calls=%async_computation.3 | async-start | bytes 11141120 | tf_op jit(solution)/shard_map/all_gather | solution.py:92
  67.3 41.0 %copy-start.1 = (bf16[96,4096]{0,1:T(8,128)(2,1)S(1)}, bf16[96,4096]{0,1:T(8,128)(2,1)}, u32[]{:S(2)}) copy-start(bf16[96,4096]{0,1:T(8,128)(2,1)} %copy.58) | copy-start | bytes 2359300
  132.6 4.0 copy-start.9
  132.6 4.8 %copy-start.8 = (s32[512,10]{0,1:T(8,128)S(1)}, s32[512,10]{0,1:T(8,128)}, u32[]{:S(2)}) copy-start(s32[512,10]{0,1:T(8,128)} %param.14) | copy-start | bytes 61444
  136.6 256.2 %all-reduce.3.cloned.1.call-start = ((), (), s32[]{:S(2)}) async-start(), calls=%async_computation.4 | async-start | bytes 16777216 | tf_op jit(solution)/shard_map/psum | solution.py:111
  137.5 27.2 %copy-start.3 = (bf16[512,1024]{1,0:T(8,128)(2,1)S(1)}, bf16[512,1024]{1,0:T(8,128)(2,1)}, u32[]{:S(2)}) copy-start(bf16[512,1024]{1,0:T(8,128)(2,1)} %param.17) | copy-start | bytes 3145732
  137.5 27.2 %copy-start.5 = (bf16[320,1024]{1,0:T(8,128)(2,1)S(1)}, bf16[320,1024]{1,0:T(8,128)(2,1)}, u32[]{:S(2)}) copy-start(bf16[320,1024]{1,0:T(8,128)(2,1)} %fusion.42) | copy-start | bytes 1966084
  137.5 27.1 %copy-start.6 = (bf16[192,1024]{1,0:T(8,128)(2,1)S(1)}, bf16[192,1024]{1,0:T(8,128)(2,1)}, u32[]{:S(2)}) copy-start(bf16[192,1024]{1,0:T(8,128)(2,1)} %fusion.45) | copy-start | bytes 1179652
  217.7 10.4 %copy-start.4 = (bf16[512,1024]{1,0:T(8,128)(2,1)S(1)}, bf16[512,1024]{1,0:T(8,128)(2,1)}, u32[]{:S(2)}) copy-start(bf16[512,1024]{1,0:T(8,128)(2,1)} %param.17) | copy-start | bytes 3145732
  231.5 2.5 copy-start.10
  392.8 4.9 %copy-start.2 = (f32[1024,1024]{1,0:T(8,128)S(1)}, f32[1024,1024]{1,0:T(8,128)}, u32[]{:S(2)}) copy-start(f32[1024,1024]{1,0:T(8,128)} %get-tuple-element.31) | copy-start | bytes 12582916
Sparse Core Ops, SparseCore 0:
  66.5 61.9 all-gather.2
  136.7 80.9 all-gather.4
  231.6 161.1 all-reduce.2

commit v6 on v5

--- a/solution.py
+++ b/solution.py
@@ -65,7 +65,11 @@
             neighbour_first.reshape(feat_size, columns_here, hidden_width),
         ],
         axis=1,
-    ).reshape(-1, hidden_width)
+    )
+    here = lax.axis_index("feat")
+    shifts = jnp.arange(feat_size, dtype=jnp.int32)
+    weights = weights[(here - shifts) % feat_size].reshape(-1, hidden_width)
+    sends = (here + shifts) % feat_size
     table = features.astype(jnp.float32).T
     lists = neighbours.T.reshape(fanout_first, feat_size, share_rows)
     own_all = features[:, :targets_part].reshape(columns_here, feat_size, share_rows)
@@ -84,7 +88,16 @@
         both = jnp.stack(
             [own_rows, mixed_rows.reshape(feat_size, piece_rows, columns_here)], axis=2
         )
-        arrived = lax.all_to_all(both, "feat", 0, 0, tiled=True)
+        rolled = both[sends]
+        arrived = jnp.stack(
+            [rolled[0]]
+            + [
+                lax.ppermute(
+                    rolled[j], "feat", [(i, (i + j) % feat_size) for i in range(feat_size)]
+                )
+                for j in range(1, feat_size)
+            ]
+        )
         lhs = jnp.transpose(arrived, (1, 0, 2, 3)).reshape(piece_rows, -1)
         pre_first = jnp.dot(lhs, weights, preferred_element_type=jnp.float32)
         part_out = jnp.maximum(pre_first, 0.0).astype(jnp.bfloat16)

time: 407 us -> 427 us (1.049)
  blocking collectives: 38.9 us -> 0 us
  local copies, waits for them, and re-layouts: 19.8 us -> 43.3 us
  starting transfers between devices: 0.12 us -> 16.9 us
  waiting for transfers between devices: 198 us -> 210 us
  other arithmetic: 30.3 us -> 38.9 us
    all_to_all x2 -> x0, blocking collectives: 38.9 us -> none  [shards(): arrived = lax.all_to_all(both, 'feat', 0, 0, tiled=True)]
    ppermute x0 -> x14, starting transfers between devices: none -> 16.8 us  [shards(): lax.ppermute(rolled[j], 'feat', [(i, (i + j) % feat_size) for i in range(...]
    unnamed x25 -> x46, local copies, waits for them, and re-layouts: 7.16 us -> 19.6 us
    ppermute x0 -> x14, waiting for transfers between devices: none -> 10.9 us  [shards(): lax.ppermute(rolled[j], 'feat', [(i, (i + j) % feat_size) for i in range(...]
    gather x0 -> x3, local copies, waits for them, and re-layouts: none -> 9.07 us  [the longest x2 4.77 us: shards(): rolled = both[sends]]
  transfers between devices with their start and end apart: 3 -> 17, of which waited for: 2 -> 6; matrix products, arithmetic and copies ran while one was open for 13% -> 17% of each run, Pallas kernels for 10% -> 10%
where the time goes in v6:
time: 427 us; the launch traced here: 426 us
  waiting for transfers between devices  210 us (49%)
  Pallas kernels  67.5 us (16%)
  local copies, waits for them, and re-layouts  43.3 us (10%)
  other arithmetic  38.9 us (9%)
  matrix products  34.8 us (8%)
  starting transfers between devices  16.9 us (4%)
  between operations  14.1 us (3%)
    psum x1, waiting for transfers between devices, shards(): lax.psum((grad_self, grad_neighbour), ('feat', 'dom'))  157 us
    pallas_call x2, Pallas kernels, gather_sum(): pl.pallas_call(kernel, out_shape=jax.ShapeDtypeStruct((count, width), jnp...  67.5 us
    all_gather x2, waiting for transfers between devices, shards(): segment = lax.all_gather(part_out, 'dom', axis=0, tiled=True)  42.1 us
    add x2, other arithmetic, shards(): sum(((flat_rows[:, k:k + 1] == table_index).astype(jnp.bfloat16) for k in...  27.2 us
    unnamed x46, local copies, waits for them, and re-layouts  19.6 us
    dot_general x2, matrix products, shards(): term = jnp.dot(counts, segment, preferred_element_type=jnp.float32)  18.9 us
    ppermute x14, starting transfers between devices, shards(): lax.ppermute(rolled[j], 'feat', [(i, (i + j) % feat_size) for i in range(...  16.8 us
    ppermute x14, waiting for transfers between devices, shards(): lax.ppermute(rolled[j], 'feat', [(i, (i + j) % feat_size) for i in range(...  10.9 us
  transfers between devices with their start and end apart: 17, of which 6 were waited for; matrix products, arithmetic and copies ran while one was open for 17% of the time, Pallas kernels for 10%

profile of v6, /device:TPU:1, one launch (start us, length us, event | category | flops | bytes accessed | tf_op | source)
XLA Modules:
  0.0 425.7 jit_solution(6435045638261901169)
XLA Ops:
  7.2 6.5 %copy.44 = f32[96,16384]{0,1:T(8,128)} copy(bf16[96,16384]{1,0:T(8,128)(2,1)} %param.9) | data formatting | bytes 9437184 | tf_op jit(solution)/shard_map/transpose | solution.py:73
  13.8 0.2 copy.55
  14.0 1.2 copy.54
  15.2 0.7 reshape_reshape.6.index_ref
  15.9 26.6 %shard_map.112 = f32[1536,96]{1,0:T(8,128)} custom-call(s32[23040]{0:T(1024)} %reshape_reshape.6.index_ref, f32[16384,96]{1,0:T(8,128)} %bitcast.135), custom_call_target="tpu_custom_call" | custom-call | tf_op jit(solution)/shard_map/pallas_call | solution.py:32
  42.5 1.9 multiply_convert_fusion.2
  44.5 1.1 copy.52
  45.5 2.1 pad_maximum_fusion.3
  47.7 2.7 gather_fusion
  50.3 2.0 slice_bitcast_fusion.7
  52.3 2.7 collective-permute-start
  55.0 1.3 collective-permute-start.1
  56.3 1.7 collective-permute-start.2
  57.9 0.3 collective-permute-start.3
  58.3 1.9 collective-permute-start.4
  60.2 3.8 pad_maximum_fusion
  64.1 4.3 %gather_fusion.1 = bf16[8,2,96,1024]{3,2,1,0:T(8,128)(2,1)} fusion(bf16[8,2,96,1024]{3,2,0,1:T(8,128)(2,1)} %pad_maximum_fusion, s32[1024]{0:T(1024)S(1)} %pad_clamp_fusion), kind=kCustom, calls=%fused_computation.1 | custom fusion | bytes 6291488 | tf_op jit(solution)/shard_map/gather | solution.py:71
  68.4 0.9 collective-permute-start.5
  69.2 1.5 bitcast_dynamic-update-slice_fusion.13
  70.8 1.6 collective-permute-start.6
  72.3 1.5 bitcast_dynamic-update-slice_fusion.12
  73.9 1.5 bitcast_dynamic-update-slice_fusion.11
  75.4 1.5 bitcast_dynamic-update-slice_fusion.10
  77.0 1.5 bitcast_dynamic-update-slice_fusion.9
  78.5 0.6 bitcast_dynamic-update-slice_fusion.8
  79.2 0.6 bitcast_dynamic-update-slice_fusion.7
  79.8 3.7 fusion.41
  83.6 0.8 slice.181
  84.4 0.3 slice.180
  84.7 1.7 reshape_reshape.7.index_ref
  86.4 40.9 %shard_map.113 = f32[2560,96]{1,0:T(8,128)} custom-call(s32[38400]{0:T(1024)} %reshape_reshape.7.index_ref, f32[16384,96]{1,0:T(8,128)} %bitcast.136), custom_call_target="tpu_custom_call" | custom-call | tf_op jit(solution)/shard_map/pallas_call | solution.py:32
  127.3 1.4 multiply_convert_fusion.1
  128.7 1.1 copy.47
  129.9 2.3 pad_maximum_fusion.1
  132.2 2.1 gather_fusion.2
  134.3 0.1 slice_bitcast_fusion
  134.4 0.3 collective-permute-start.7
  134.7 0.5 collective-permute-start.8
  135.2 1.3 collective-permute-start.9
  136.6 1.9 collective-permute-start.10
  138.5 2.4 collective-permute-start.11
  140.9 3.3 collective-permute-done.8
  144.2 6.4 %collective-permute-done.9 = bf16[320,2,96]{0,2,1:T(8,128)(2,1)S(1)} collective-permute-done((bf16[320,2,96]{0,2,1:T(8,128)(2,1)S(1)}, bf16[320,2,96]{0,2,1:T(8,128)(2,1)S(1)}, u32[]{:S(2)}, u32[]{:S(2)}) %collective-permute-start.9) | collective-permute-done | bytes 122912 | tf_op jit(solution)/shard_map/ppermute | solution.py:95
  150.8 0.4 collective-permute-done.12
  151.2 0.8 collective-permute-done.13
  152.0 2.0 fusion.39
  154.3 0.2 mul.19
  154.5 0.1 copy.49
  154.6 0.2 mul.16
  154.8 0.1 copy.48
  155.0 10.5 %fusion.29 = bf16[512,3072]{1,0:T(8,128)(2,1)} fusion(s32[512]{0:T(512)S(1)} %bitcast.150, s32[512]{0:T(512)S(1)} %bitcast.151, s32[512]{0:T(512)S(1)} %bitcast.152, s32[512]{0:T(512)S(1)} %bitcast.153, s32[512]{0:T(512)S(1)} %bitcast.154, s32[512]{0:T(512)S(1)} %bitcast.155, s32[512]{0:T(512)S(1)} %bitcast.156, s32[512]{0:T(512)S(1)} %bitcast.157, ...), kind=kLoop, calls=%fused_computation.52 | loop fusion | flops 62914560 | bytes 3166208 | tf_op jit(solution)/shard_map/add | solution.py:109
  165.5 16.7 %fusion.20 = bf16[512,5120]{1,0:T(8,128)(2,1)} fusion(s32[512]{0:T(512)S(1)} %bitcast.160, s32[512]{0:T(512)S(1)} %bitcast.161, s32[512]{0:T(512)S(1)} %bitcast.162, s32[512]{0:T(512)S(1)} %bitcast.163, s32[512]{0:T(512)S(1)} %bitcast.164, s32[512]{0:T(512)S(1)} %bitcast.165, s32[512]{0:T(512)S(1)} %bitcast.166, s32[512]{0:T(512)S(1)} %bitcast.167, ...), kind=kLoop, calls=%fused_computation.43 | loop fusion | flops 104857600 | bytes 5263360 | tf_op jit(solution)/shard_map/add | solution.py:109
  182.2 3.3 fusion.44
  185.5 8.5 %fusion.54 = f32[512,1024]{1,0:T(8,128)} fusion(bf16[512,3072]{1,0:T(8,128)(2,1)} %fusion.29, bf16[3072,1024]{1,0:T(8,128)(2,1)} %all-gather.3.cloned.1.call-done), kind=kOutput, calls=%fused_computation.132 | convolution fusion | flops 3221225472 | bytes 11534336 | tf_op jit(solution)/shard_map/dot_general | solution.py:114
  194.0 42.1 %all-gather.5.cloned.1.call-done = bf16[5120,1024]{1,0:T(8,128)(2,1)} async-done(((bf16[320,1024]{1,0:T(8,128)(2,1)}), bf16[5120,1024]{1,0:T(8,128)(2,1)}) %all-gather.5.cloned.1.call-update) | async-done | bytes 10485776 | tf_op jit(solution)/shard_map/all_gather | solution.py:105
  236.1 10.4 %multiply_convert_fusion = bf16[512,1024]{1,0:T(8,128)(2,1)S(1)} fusion(f32[512,1024]{1,0:T(8,128)} %fusion.54, bf16[512,5120]{1,0:T(8,128)(2,1)} %fusion.20, bf16[5120,1024]{1,0:T(8,128)(2,1)} %all-gather.5.cloned.1.call-done), kind=kOutput, calls=%fused_computation.63 | convolution fusion | flops 5370281984 | bytes 18874368 | tf_op jit(solution)/shard_map/dot_general | solution.py:114
  246.5 1.0 copy-done.5
  247.5 3.3 fusion.55
  250.9 1.2 fusion.45
  252.1 0.6 copy-done.13
  252.8 2.2 add_convert_fusion
  255.0 157.2 %all-reduce.3.cloned.1.call-done = (f32[1024,1024]{1,0:T(8,128)}, f32[1024,1024]{1,0:T(8,128)}) async-done(((f32[1024,1024]{1,0:T(8,128)}, f32[1024,1024]{1,0:T(8,128)}), (f32[1024,1024]{1,0:T(8,128)}, f32[1024,1024]{1,0:T(8,128)})) %all-reduce.3.cloned.1.call-update) | async-done | bytes 8388624 | tf_op jit(solution)/shard_map/psum | solution.py:124
  412.2 4.9 %copy.74 = f32[1024,1024]{1,0:T(8,128)} copy(f32[1024,1024]{1,0:T(8,128)} %get-tuple-element.48) | data formatting | bytes 8388608
  417.1 2.0 copy.75
  (64 shorter events, 0.7 us)
Async XLA Ops:
  7.2 243.7 %copy-start = (bf16[1024,1024]{1,0:T(8,128)(2,1)S(1)}, bf16[1024,1024]{1,0:T(8,128)(2,1)}, u32[]{:S(2)}) copy-start(bf16[1024,1024]{1,0:T(8,128)(2,1)} %param.15) | copy-start | bytes 6291460
  7.2 178.3 %all-gather.3.cloned.1.call-start = ((), (), s32[]{:S(2)}) async-start(), calls=%async_computation | async-start | bytes 6684672 | tf_op jit(solution)/shard_map/all_gather | solution.py:105
  7.2 6.6 %copy-start.10 = (s32[4096,15]{0,1:T(8,128)S(1)}, s32[4096,15]{0,1:T(8,128)}, u32[]{:S(2)}) copy-start(s32[4096,15]{0,1:T(8,128)} %param.10) | copy-start | bytes 737284
  7.2 6.7 %slice-start = ((bf16[96,16384]{1,0:T(8,128)(2,1)}), bf16[96,4096]{1,0:T(8,128)(2,1)S(1)}, s32[]{:S(2)}) async-start(bf16[96,16384]{1,0:T(8,128)(2,1)} %param.9), calls=%async_computation.3 | async-start | bytes 1572864 | tf_op jit(solution)/shard_map/slice | solution.py:75
  15.9 28.5 %copy-start.3 = (bf16[12,8,8,512]{3,2,1,0:T(8,128)(2,1)S(1)}, bf16[12,8,8,512]{3,2,1,0:T(8,128)(2,1)}, u32[]{:S(2)}) copy-start(bf16[12,8,8,512]{3,2,1,0:T(8,128)(2,1)} %copy.54) | copy-start | bytes 2359300
  52.3 16.1 %collective-permute-start = (bf16[192,2,96]{2,0,1:T(8,128)(2,1)}, bf16[192,2,96]{2,0,1:T(8,128)(2,1)}, u32[]{:S(2)}, u32[]{:S(2)}) collective-permute-start(bf16[192,2,96]{2,0,1:T(8,128)(2,1)} %get-tuple-element.21), channel_id=1, source_target_pairs={{0,16},{16,32},{32,48},{48,64},{64,80},{80,96},{96,112},{112,0},{1... | collective-permute-start | bytes 221192 | tf_op jit(solution)/shard_map/ppermute | solution.py:95
  55.0 15.8 %collective-permute-start.1 = (bf16[192,2,96]{2,0,1:T(8,128)(2,1)}, bf16[192,2,96]{2,0,1:T(8,128)(2,1)}, u32[]{:S(2)}, u32[]{:S(2)}) collective-permute-start(bf16[192,2,96]{2,0,1:T(8,128)(2,1)} %get-tuple-element.20), channel_id=1, source_target_pairs={{0,32},{16,48},{32,64},{48,80},{64,96},{80,112},{96,0},{112,16},{1... | collective-permute-start | bytes 221192 | tf_op jit(solution)/shard_map/ppermute | solution.py:95
  56.3 17.6 %collective-permute-start.2 = (bf16[192,2,96]{2,0,1:T(8,128)(2,1)}, bf16[192,2,96]{2,0,1:T(8,128)(2,1)}, u32[]{:S(2)}, u32[]{:S(2)}) collective-permute-start(bf16[192,2,96]{2,0,1:T(8,128)(2,1)} %get-tuple-element.19), channel_id=1, source_target_pairs={{0,48},{16,64},{32,80},{48,96},{64,112},{80,0},{96,16},{112,32},{1... | collective-permute-start | bytes 221192 | tf_op jit(solution)/shard_map/ppermute | solution.py:95
  57.9 17.5 %collective-permute-start.3 = (bf16[192,2,96]{2,0,1:T(8,128)(2,1)S(1)}, bf16[192,2,96]{2,0,1:T(8,128)(2,1)}, u32[]{:S(2)}, u32[]{:S(2)}) collective-permute-start(bf16[192,2,96]{2,0,1:T(8,128)(2,1)S(1)} %get-tuple-element.18), channel_id=1, source_target_pairs={{0,64},{16,80},{32,96},{48,112},{64,0},{80,16},{96,32},{112,48},{1... | collective-permute-start | bytes 221192 | tf_op jit(solution)/shard_map/ppermute | solution.py:95
  58.3 18.7 %collective-permute-start.4 = (bf16[192,2,96]{2,0,1:T(8,128)(2,1)S(1)}, bf16[192,2,96]{2,0,1:T(8,128)(2,1)}, u32[]{:S(2)}, u32[]{:S(2)}) collective-permute-start(bf16[192,2,96]{2,0,1:T(8,128)(2,1)S(1)} %get-tuple-element.17), channel_id=1, source_target_pairs={{0,80},{16,96},{32,112},{48,0},{64,16},{80,32},{96,48},{112,64},{1... | collective-permute-start | bytes 221192 | tf_op jit(solution)/shard_map/ppermute | solution.py:95
  68.4 10.1 %collective-permute-start.5 = (bf16[192,2,96]{2,0,1:T(8,128)(2,1)S(1)}, bf16[192,2,96]{2,0,1:T(8,128)(2,1)S(1)}, u32[]{:S(2)}, u32[]{:S(2)}) collective-permute-start(bf16[192,2,96]{2,0,1:T(8,128)(2,1)S(1)} %get-tuple-element.16), channel_id=1, source_target_pairs={{0,96},{16,112},{32,0},{48,16},{64,32},{80,48},{96,64},{112,80},{1... | collective-permute-start | bytes 221192 | tf_op jit(solution)/shard_map/ppermute | solution.py:95
  70.8 8.4 %collective-permute-start.6 = (bf16[192,2,96]{2,0,1:T(8,128)(2,1)S(1)}, bf16[192,2,96]{2,0,1:T(8,128)(2,1)S(1)}, u32[]{:S(2)}, u32[]{:S(2)}) collective-permute-start(bf16[192,2,96]{2,0,1:T(8,128)(2,1)S(1)} %get-tuple-element.15), channel_id=1, source_target_pairs={{0,112},{16,0},{32,16},{48,32},{64,48},{80,64},{96,80},{112,96},{1... | collective-permute-start | bytes 221192 | tf_op jit(solution)/shard_map/ppermute | solution.py:95
  83.6 152.5 %all-gather.5.cloned.1.call-start = ((), (), s32[]{:S(2)}) async-start(), calls=%async_computation.1 | async-start | bytes 11141120 | tf_op jit(solution)/shard_map/all_gather | solution.py:105
  134.3 17.7 %copy-start.1 = (bf16[8,2,96,1024]{3,2,1,0:T(8,128)(2,1)S(1)}, bf16[8,2,96,1024]{3,2,1,0:T(8,128)(2,1)}, u32[]{:S(2)}) copy-start(bf16[8,2,96,1024]{3,2,1,0:T(8,128)(2,1)} %gather_fusion.1) | copy-start | bytes 9437188
  134.4 6.5 %collective-permute-start.7 = (bf16[320,2,96]{0,2,1:T(8,128)(2,1)S(1)}, bf16[320,2,96]{0,2,1:T(8,128)(2,1)S(1)}, u32[]{:S(2)}, u32[]{:S(2)}) collective-permute-start(bf16[320,2,96]{0,2,1:T(8,128)(2,1)S(1)} %get-tuple-element.13), channel_id=1, source_target_pairs={{0,16},{16,32},{32,48},{48,64},{64,80},{80,96},{96,112},{112,0},{1... | collective-permute-start | bytes 368648 | tf_op jit(solution)/shard_map/ppermute | solution.py:95
  134.7 9.5 %collective-permute-start.8 = (bf16[320,2,96]{0,2,1:T(8,128)(2,1)S(1)}, bf16[320,2,96]{0,2,1:T(8,128)(2,1)S(1)}, u32[]{:S(2)}, u32[]{:S(2)}) collective-permute-start(bf16[320,2,96]{0,2,1:T(8,128)(2,1)S(1)} %get-tuple-element.12), channel_id=1, source_target_pairs={{0,32},{16,48},{32,64},{48,80},{64,96},{80,112},{96,0},{112,16},{1... | collective-permute-start | bytes 368648 | tf_op jit(solution)/shard_map/ppermute | solution.py:95
  135.2 15.4 %collective-permute-start.9 = (bf16[320,2,96]{0,2,1:T(8,128)(2,1)S(1)}, bf16[320,2,96]{0,2,1:T(8,128)(2,1)S(1)}, u32[]{:S(2)}, u32[]{:S(2)}) collective-permute-start(bf16[320,2,96]{0,2,1:T(8,128)(2,1)S(1)} %get-tuple-element.11), channel_id=1, source_target_pairs={{0,48},{16,64},{32,80},{48,96},{64,112},{80,0},{96,16},{112,32},{1... | collective-permute-start | bytes 368648 | tf_op jit(solution)/shard_map/ppermute | solution.py:95
  136.6 14.1 %collective-permute-start.10 = (bf16[320,2,96]{0,2,1:T(8,128)(2,1)S(1)}, bf16[320,2,96]{0,2,1:T(8,128)(2,1)S(1)}, u32[]{:S(2)}, u32[]{:S(2)}) collective-permute-start(bf16[320,2,96]{0,2,1:T(8,128)(2,1)S(1)} %get-tuple-element.10), channel_id=1, source_target_pairs={{0,64},{16,80},{32,96},{48,112},{64,0},{80,16},{96,32},{112,48},{1... | collective-permute-start | bytes 368648 | tf_op jit(solution)/shard_map/ppermute | solution.py:95
  138.5 12.2 %collective-permute-start.11 = (bf16[320,2,96]{0,2,1:T(8,128)(2,1)S(1)}, bf16[320,2,96]{0,2,1:T(8,128)(2,1)S(1)}, u32[]{:S(2)}, u32[]{:S(2)}) collective-permute-start(bf16[320,2,96]{0,2,1:T(8,128)(2,1)S(1)} %get-tuple-element.9), channel_id=1, source_target_pairs={{0,80},{16,96},{32,112},{48,0},{64,16},{80,32},{96,48},{112,64},{1... | collective-permute-start | bytes 368648 | tf_op jit(solution)/shard_map/ppermute | solution.py:95
  140.9 10.3 %collective-permute-start.12 = (bf16[320,2,96]{0,2,1:T(8,128)(2,1)S(1)}, bf16[320,2,96]{0,2,1:T(8,128)(2,1)S(1)}, u32[]{:S(2)}, u32[]{:S(2)}) collective-permute-start(bf16[320,2,96]{0,2,1:T(8,128)(2,1)S(1)} %get-tuple-element.8), channel_id=1, source_target_pairs={{0,96},{16,112},{32,0},{48,16},{64,32},{80,48},{96,64},{112,80},{1... | collective-permute-start | bytes 368648 | tf_op jit(solution)/shard_map/ppermute | solution.py:95
  144.2 7.8 %collective-permute-start.13 = (bf16[320,2,96]{0,2,1:T(8,128)(2,1)S(1)}, bf16[320,2,96]{0,2,1:T(8,128)(2,1)S(1)}, u32[]{:S(2)}, u32[]{:S(2)}) collective-permute-start(bf16[320,2,96]{0,2,1:T(8,128)(2,1)S(1)} %get-tuple-element.7), channel_id=1, source_target_pairs={{0,112},{16,0},{32,16},{48,32},{64,48},{80,64},{96,80},{112,96},{1... | collective-permute-start | bytes 368648 | tf_op jit(solution)/shard_map/ppermute | solution.py:95
  150.8 3.4 copy-start.12
  152.0 2.9 copy-start.11
  154.1 258.1 %all-reduce.3.cloned.1.call-start = ((), (), s32[]{:S(2)}) async-start(), calls=%async_computation.2 | async-start | bytes 16777216 | tf_op jit(solution)/shard_map/psum | solution.py:124
  165.5 16.7 %copy-start.4 = (bf16[320,1024]{1,0:T(8,128)(2,1)S(1)}, bf16[320,1024]{1,0:T(8,128)(2,1)}, u32[]{:S(2)}) copy-start(bf16[320,1024]{1,0:T(8,128)(2,1)} %fusion.39) | copy-start | bytes 1966084
  165.5 16.7 %copy-start.7 = (bf16[512,1024]{1,0:T(8,128)(2,1)S(1)}, bf16[512,1024]{1,0:T(8,128)(2,1)}, u32[]{:S(2)}) copy-start(bf16[512,1024]{1,0:T(8,128)(2,1)} %param.17) | copy-start | bytes 3145732
  165.5 16.7 %copy-start.9 = (bf16[192,1024]{1,0:T(8,128)(2,1)S(1)}, bf16[192,1024]{1,0:T(8,128)(2,1)}, u32[]{:S(2)}) copy-start(bf16[192,1024]{1,0:T(8,128)(2,1)} %fusion.41) | copy-start | bytes 1179652
  236.1 11.4 %copy-start.8 = (bf16[512,1024]{1,0:T(8,128)(2,1)S(1)}, bf16[512,1024]{1,0:T(8,128)(2,1)}, u32[]{:S(2)}) copy-start(bf16[512,1024]{1,0:T(8,128)(2,1)} %param.17) | copy-start | bytes 3145732
  246.5 1.0 copy-start.5
  250.8 1.3 copy-start.6
  250.9 1.9 copy-start.13
  412.2 4.9 %copy-start.2 = (f32[1024,1024]{1,0:T(8,128)S(1)}, f32[1024,1024]{1,0:T(8,128)}, u32[]{:S(2)}) copy-start(f32[1024,1024]{1,0:T(8,128)} %get-tuple-element.49) | copy-start | bytes 12582916
Sparse Core Ops, SparseCore 0:
  83.7 61.2 all-gather.2
  154.2 81.8 all-gather.4
  251.0 161.1 all-reduce.2

commit v7 on v5

--- a/solution.py
+++ b/solution.py
@@ -12,8 +12,9 @@
     )
 
 
-def gather_sum(table, index, block=512, unroll=8):
+def gather_sum(table, index, unroll=8):
     fanout, count = index.shape
+    block = 512 if count % 512 == 0 else 256
     rows, width = table.shape
 
     def kernel(index_ref, table_ref, out_ref):
@@ -58,7 +59,7 @@
     hidden_width = self_first.shape[1]
     feat_size = lax.axis_size("feat")
     share_rows = targets_part // feat_size
-    cuts = [0, 3 * share_rows // 8, share_rows]
+    cuts = [0, 7 * share_rows // 16, share_rows]
     weights = jnp.stack(
         [
             self_first.reshape(feat_size, columns_here, hidden_width),

time: 407 us -> 415 us (1.020)
  waiting for transfers between devices: 198 us -> 205 us
    all_gather x2, waiting for transfers between devices: 41.2 us -> 48.4 us  [shards(): segment = lax.all_gather(part_out, 'dom', axis=0, tiled=True)]
    unnamed x25 -> x36, local copies, waits for them, and re-layouts: 7.16 us -> 10.3 us
  transfers between devices with their start and end apart: 3 -> 3, of which waited for: 2 -> 2; matrix products, arithmetic and copies ran while one was open for 13% -> 13% of each run, Pallas kernels for 10% -> 7%
where the time goes in v7:
time: 415 us; the launch traced here: 414 us
  waiting for transfers between devices  205 us (49%)
  Pallas kernels  67.6 us (16%)
  blocking collectives  37.8 us (9%)
  matrix products  36.3 us (9%)
  other arithmetic  32.3 us (8%)
  local copies, waits for them, and re-layouts  21.3 us (5%)
  between operations  14 us (3%)
    psum x1, waiting for transfers between devices, shards(): lax.psum((grad_self, grad_neighbour), ('feat', 'dom'))  156 us
    pallas_call x2, Pallas kernels, gather_sum(): pl.pallas_call(kernel, out_shape=jax.ShapeDtypeStruct((count, width), jnp...  67.6 us
    all_gather x2, waiting for transfers between devices, shards(): segment = lax.all_gather(part_out, 'dom', axis=0, tiled=True)  48.4 us
    all_to_all x2, blocking collectives, shards(): arrived = lax.all_to_all(both, 'feat', 0, 0, tiled=True)  37.8 us
    add x2, other arithmetic, shards(): sum(((flat_rows[:, k:k + 1] == table_index).astype(jnp.bfloat16) for k in...  26.9 us
    dot_general x2, matrix products, shards(): term = jnp.dot(counts, segment, preferred_element_type=jnp.float32)  19.1 us
    unnamed x36, local copies, waits for them, and re-layouts  10.3 us
  transfers between devices with their start and end apart: 3, of which 2 were waited for; matrix products, arithmetic and copies ran while one was open for 13% of the time, Pallas kernels for 7%

profile of v7, /device:TPU:1, one launch (start us, length us, event | category | flops | bytes accessed | tf_op | source)
XLA Modules:
  0.0 414.5 jit_solution(16707060688029427261)
XLA Ops:
  7.2 0.0 copy-start
  7.2 0.0 copy-start.9
  7.2 0.0 all-gather.5.cloned.1.call-start
  7.2 6.5 %copy.47 = f32[96,16384]{0,1:T(8,128)} copy(bf16[96,16384]{1,0:T(8,128)(2,1)} %param.9) | data formatting | bytes 9437184 | tf_op jit(solution)/shard_map/transpose | solution.py:70
  13.7 0.0 copy-done.9
  13.7 0.2 copy.58
  13.9 0.0 copy-start.4
  13.9 0.7 copy-done.4
  14.6 0.1 slice.103
  14.7 0.8 reshape_reshape.7.index_ref
  15.5 37.5 %shard_map.113 = f32[2304,96]{1,0:T(8,128)} custom-call(s32[34560]{0:T(1024)} %reshape_reshape.7.index_ref, f32[16384,96]{1,0:T(8,128)} %bitcast.73), custom_call_target="tpu_custom_call" | custom-call | tf_op jit(solution)/shard_map/pallas_call | solution.py:33
  53.0 1.4 multiply_convert_fusion.1
  54.4 0.0 slice-done
  54.4 0.3 copy.57
  54.6 0.0 copy-start.2
  54.7 0.9 copy-done.2
  55.5 0.3 slice.102
  55.8 1.2 copy.56
  57.0 1.4 pad_maximum_fusion.15
  58.5 22.3 %all_to_all.10 = bf16[8,288,2,96]{3,1,2,0:T(8,128)(2,1)S(1)} all-to-all(bf16[8,288,2,96]{3,1,2,0:T(8,128)(2,1)S(1)} %pad_maximum_fusion.15), channel_id=1, replica_groups=mesh['feat'=8,'dom'=16] {'feat'}, dimensions={0} | all-to-all | bytes 1769472 | tf_op jit(solution)/shard_map/all_to_all | solution.py:88
  80.7 0.0 copy-done.13
  80.8 0.0 copy-done.14
  80.8 2.0 fusion.43
  82.7 0.0 all-gather.5.cloned.1.call-update
  82.8 0.0 all-gather.3.cloned.1.call-start
  82.8 0.9 slice.101
  83.7 0.0 copy-done.3
  83.8 0.8 reshape_reshape.6.index_ref
  84.5 30.1 %shard_map.112 = f32[1792,96]{1,0:T(8,128)} custom-call(s32[26880]{0:T(1024)} %reshape_reshape.6.index_ref, f32[16384,96]{1,0:T(8,128)} %bitcast.74), custom_call_target="tpu_custom_call" | custom-call | tf_op jit(solution)/shard_map/pallas_call | solution.py:33
  114.6 1.2 multiply_convert_fusion.2
  115.9 1.0 copy.48
  116.8 0.1 copy.60
  116.9 1.2 pad_maximum_fusion.17
  118.1 15.5 %all_to_all.11 = bf16[8,224,2,96]{1,3,2,0:T(8,128)(2,1)S(1)} all-to-all(bf16[8,224,2,96]{1,3,2,0:T(8,128)(2,1)S(1)} %pad_maximum_fusion.17), channel_id=1, replica_groups=mesh['feat'=8,'dom'=16] {'feat'}, dimensions={0} | all-to-all | bytes 1376256 | tf_op jit(solution)/shard_map/all_to_all | solution.py:88
  133.6 3.7 fusion.45
  137.3 0.0 all-gather.3.cloned.1.call-update
  137.4 0.2 all-reduce.3.cloned.1.call-start
  137.6 0.0 copy-done.11
  137.6 0.1 multiply_reduce_fusion.1
  137.7 0.2 mul.16
  137.9 0.1 copy.51
  138.1 0.2 mul.19
  138.3 0.1 copy.52
  138.4 0.0 copy-done.10
  138.5 0.0 copy-start.5
  138.5 0.0 copy-start.7
  138.5 0.0 copy-start.8
  138.5 15.1 %fusion.20 = bf16[512,4608]{1,0:T(8,128)(2,1)} fusion(s32[512]{0:T(512)S(1)} %bitcast.86, s32[512]{0:T(512)S(1)} %bitcast.87, s32[512]{0:T(512)S(1)} %bitcast.88, s32[512]{0:T(512)S(1)} %bitcast.89, s32[512]{0:T(512)S(1)} %bitcast.90, s32[512]{0:T(512)S(1)} %bitcast.91, s32[512]{0:T(512)S(1)} %bitcast.92, s32[512]{0:T(512)S(1)} %bitcast.93, ...), kind=kLoop, calls=%fused_computation.40 | loop fusion | flops 94371840 | bytes 4739072 | tf_op jit(solution)/shard_map/add | solution.py:97
  153.6 11.9 %fusion.29 = bf16[512,3584]{1,0:T(8,128)(2,1)} fusion(s32[512]{0:T(512)S(1)} %bitcast.96, s32[512]{0:T(512)S(1)} %bitcast.97, s32[512]{0:T(512)S(1)} %bitcast.98, s32[512]{0:T(512)S(1)} %bitcast.99, s32[512]{0:T(512)S(1)} %bitcast.100, s32[512]{0:T(512)S(1)} %bitcast.101, s32[512]{0:T(512)S(1)} %bitcast.102, s32[512]{0:T(512)S(1)} %bitcast.103, ...), kind=kLoop, calls=%fused_computation.49 | loop fusion | flops 73400320 | bytes 3690496 | tf_op jit(solution)/shard_map/add | solution.py:97
  165.5 0.0 copy-done.5
  165.5 0.0 copy-done.7
  165.5 3.3 fusion.48
  168.8 10.4 %fusion.56 = f32[512,1024]{1,0:T(8,128)} fusion(bf16[512,4608]{1,0:T(8,128)(2,1)} %fusion.20, bf16[4608,1024]{1,0:T(8,128)(2,1)} %all-gather.5.cloned.1.call-done), kind=kOutput, calls=%fused_computation.89 | convolution fusion | flops 4831838208 | bytes 16252928 | tf_op jit(solution)/shard_map/dot_general | solution.py:102
  179.1 48.4 %all-gather.3.cloned.1.call-done = bf16[3584,1024]{1,0:T(8,128)(2,1)} async-done(((bf16[224,1024]{1,0:T(8,128)(2,1)}), bf16[3584,1024]{1,0:T(8,128)(2,1)}) %all-gather.3.cloned.1.call-update) | async-done | bytes 7340048 | tf_op jit(solution)/shard_map/all_gather | solution.py:93
  227.5 8.8 %multiply_convert_fusion = bf16[512,1024]{1,0:T(8,128)(2,1)S(1)} fusion(f32[512,1024]{1,0:T(8,128)} %fusion.56, bf16[512,3584]{1,0:T(8,128)(2,1)} %fusion.29, bf16[3584,1024]{1,0:T(8,128)(2,1)} %all-gather.3.cloned.1.call-done), kind=kOutput, calls=%fused_computation.60 | convolution fusion | flops 3759669248 | bytes 14155776 | tf_op jit(solution)/shard_map/dot_general | solution.py:102
  236.3 3.3 fusion.57
  239.6 0.0 all-reduce.3.cloned.1.call-update
  239.7 0.0 copy-start.12
  239.7 2.6 fusion.49
  242.3 0.0 copy-done.12
  242.3 2.3 add_convert_fusion
  244.5 156.4 %all-reduce.3.cloned.1.call-done = (f32[1024,1024]{1,0:T(8,128)}, f32[1024,1024]{1,0:T(8,128)}) async-done(((f32[1024,1024]{1,0:T(8,128)}, f32[1024,1024]{1,0:T(8,128)}), (f32[1024,1024]{1,0:T(8,128)}, f32[1024,1024]{1,0:T(8,128)})) %all-reduce.3.cloned.1.call-update) | async-done | bytes 8388624 | tf_op jit(solution)/shard_map/psum | solution.py:112
  401.0 4.9 %copy.63 = f32[1024,1024]{1,0:T(8,128)} copy(f32[1024,1024]{1,0:T(8,128)} %get-tuple-element.30) | data formatting | bytes 8388608
  405.9 2.0 copy.64
  (17 shorter events, 0.1 us)
Async XLA Ops:
  7.2 232.5 %copy-start = (bf16[1024,1024]{1,0:T(8,128)(2,1)S(1)}, bf16[1024,1024]{1,0:T(8,128)(2,1)}, u32[]{:S(2)}) copy-start(bf16[1024,1024]{1,0:T(8,128)(2,1)} %param.15) | copy-start | bytes 6291460
  7.2 6.5 %copy-start.9 = (s32[4096,15]{0,1:T(8,128)S(1)}, s32[4096,15]{0,1:T(8,128)}, u32[]{:S(2)}) copy-start(s32[4096,15]{0,1:T(8,128)} %param.10) | copy-start | bytes 737284
  7.2 161.6 %all-gather.5.cloned.1.call-start = ((), (), s32[]{:S(2)}) async-start(), calls=%async_computation.3 | async-start | bytes 10027008 | tf_op jit(solution)/shard_map/all_gather | solution.py:93
  13.9 0.7 copy-start.4
  15.5 38.9 %slice-start = ((bf16[96,16384]{1,0:T(8,128)(2,1)}), bf16[96,4096]{1,0:T(8,128)(2,1)S(1)}, s32[]{:S(2)}) async-start(bf16[96,16384]{1,0:T(8,128)(2,1)} %param.9), calls=%async_computation.5 | async-start | bytes 1572864 | tf_op jit(solution)/shard_map/slice | solution.py:72
  54.6 0.9 copy-start.2
  57.0 23.7 %copy-start.13 = (bf16[768,1024]{1,0:T(8,128)(2,1)S(1)}, bf16[768,1024]{1,0:T(8,128)(2,1)}, u32[]{:S(2)}) copy-start(bf16[768,1024]{1,0:T(8,128)(2,1)} %param.12) | copy-start | bytes 4718596
  57.0 23.7 %copy-start.14 = (bf16[768,1024]{1,0:T(8,128)(2,1)S(1)}, bf16[768,1024]{1,0:T(8,128)(2,1)}, u32[]{:S(2)}) copy-start(bf16[768,1024]{1,0:T(8,128)(2,1)} %param.11) | copy-start | bytes 4718596
  80.8 3.0 copy-start.3
  82.8 144.8 %all-gather.3.cloned.1.call-start = ((), (), s32[]{:S(2)}) async-start(), calls=%async_computation.2 | async-start | bytes 7798784 | tf_op jit(solution)/shard_map/all_gather | solution.py:93
  133.6 4.0 copy-start.11
  133.6 4.8 %copy-start.10 = (s32[512,10]{0,1:T(8,128)S(1)}, s32[512,10]{0,1:T(8,128)}, u32[]{:S(2)}) copy-start(s32[512,10]{0,1:T(8,128)} %param.14) | copy-start | bytes 61444
  137.4 263.6 %all-reduce.3.cloned.1.call-start = ((), (), s32[]{:S(2)}) async-start(), calls=%async_computation.4 | async-start | bytes 16777216 | tf_op jit(solution)/shard_map/psum | solution.py:112
  138.5 27.0 %copy-start.5 = (bf16[512,1024]{1,0:T(8,128)(2,1)S(1)}, bf16[512,1024]{1,0:T(8,128)(2,1)}, u32[]{:S(2)}) copy-start(bf16[512,1024]{1,0:T(8,128)(2,1)} %param.17) | copy-start | bytes 3145732
  138.5 27.0 %copy-start.7 = (bf16[288,1024]{1,0:T(8,128)(2,1)S(1)}, bf16[288,1024]{1,0:T(8,128)(2,1)}, u32[]{:S(2)}) copy-start(bf16[288,1024]{1,0:T(8,128)(2,1)} %fusion.43) | copy-start | bytes 1769476
  138.5 27.0 %copy-start.8 = (bf16[224,1024]{1,0:T(8,128)(2,1)S(1)}, bf16[224,1024]{1,0:T(8,128)(2,1)}, u32[]{:S(2)}) copy-start(bf16[224,1024]{1,0:T(8,128)(2,1)} %fusion.45) | copy-start | bytes 1376260
  227.5 8.8 %copy-start.6 = (bf16[512,1024]{1,0:T(8,128)(2,1)S(1)}, bf16[512,1024]{1,0:T(8,128)(2,1)}, u32[]{:S(2)}) copy-start(bf16[512,1024]{1,0:T(8,128)(2,1)} %param.17) | copy-start | bytes 3145732
  239.7 2.6 copy-start.12
  401.0 4.9 %copy-start.1 = (f32[1024,1024]{1,0:T(8,128)S(1)}, f32[1024,1024]{1,0:T(8,128)}, u32[]{:S(2)}) copy-start(f32[1024,1024]{1,0:T(8,128)} %get-tuple-element.31) | copy-start | bytes 12582916
Sparse Core Ops, SparseCore 0:
  82.9 76.0 all-gather.4
  161.7 65.8 all-gather.2
  239.8 161.1 all-reduce.2

commit v8 on v5

--- a/solution.py
+++ b/solution.py
@@ -12,7 +12,7 @@
     )
 
 
-def gather_sum(table, index, block=512, unroll=8):
+def gather_sum(table, index, block=512, unroll=16):
     fanout, count = index.shape
     rows, width = table.shape
 

time: 407 us -> 405 us (level)
  no operation moved by 1% of the time
where the time goes in v8:
time: 405 us; the launch traced here: 404 us
  waiting for transfers between devices  198 us (49%)
  Pallas kernels  65.6 us (16%)
  blocking collectives  38.9 us (10%)
  matrix products  37.7 us (9%)
  other arithmetic  30.3 us (7%)
  local copies, waits for them, and re-layouts  19.8 us (5%)
  between operations  14 us (3%)
    psum x1, waiting for transfers between devices, shards(): lax.psum((grad_self, grad_neighbour), ('feat', 'dom'))  157 us
    pallas_call x2, Pallas kernels, gather_sum(): pl.pallas_call(kernel, out_shape=jax.ShapeDtypeStruct((count, width), jnp...  65.6 us
    all_gather x2, waiting for transfers between devices, shards(): segment = lax.all_gather(part_out, 'dom', axis=0, tiled=True)  41.2 us
    all_to_all x2, blocking collectives, shards(): arrived = lax.all_to_all(both, 'feat', 0, 0, tiled=True)  38.9 us
    add x2, other arithmetic, shards(): sum(((flat_rows[:, k:k + 1] == table_index).astype(jnp.bfloat16) for k in...  27.1 us
    dot_general x2, matrix products, shards(): term = jnp.dot(counts, segment, preferred_element_type=jnp.float32)  18.9 us
  transfers between devices with their start and end apart: 3, of which 2 were waited for; matrix products, arithmetic and copies ran while one was open for 13% of the time, Pallas kernels for 10%

profile of v8, /device:TPU:1, one launch (start us, length us, event | category | flops | bytes accessed | tf_op | source)
XLA Modules:
  0.0 404.2 jit_solution(11318535548204934545)
XLA Ops:
  7.2 0.0 copy-start
  7.2 0.0 copy-start.7
  7.2 0.0 all-gather.3.cloned.1.call-start
  7.2 6.5 %copy.59 = f32[96,16384]{0,1:T(8,128)} copy(bf16[96,16384]{1,0:T(8,128)(2,1)} %param.9) | data formatting | bytes 9437184 | tf_op jit(solution)/shard_map/transpose | solution.py:69
  13.7 0.0 copy-done.7
  13.7 0.2 copy.66
  13.9 0.7 reshape_reshape.6.index_ref
  14.7 0.0 slice-start
  14.7 25.8 %shard_map.112 = f32[1536,96]{1,0:T(8,128)} custom-call(s32[23040]{0:T(1024)} %reshape_reshape.6.index_ref, f32[16384,96]{1,0:T(8,128)} %bitcast.72), custom_call_target="tpu_custom_call" | custom-call | tf_op jit(solution)/shard_map/pallas_call | solution.py:32
  40.5 1.2 multiply_convert_fusion.2
  41.7 0.0 slice-done
  41.7 1.3 copy.58
  43.0 1.0 slice_bitcast_fusion.1
  44.0 0.2 pad_maximum_fusion.17
  44.2 17.9 %all_to_all.10 = bf16[8,192,2,96]{3,1,2,0:T(8,128)(2,1)S(1)} all-to-all(bf16[8,192,2,96]{3,1,2,0:T(8,128)(2,1)S(1)} %pad_maximum_fusion.17), channel_id=1, replica_groups=mesh['feat'=8,'dom'=16] {'feat'}, dimensions={0} | all-to-all | bytes 1179648 | tf_op jit(solution)/shard_map/all_to_all | solution.py:87
  62.0 3.5 fusion.45
  65.5 0.0 all-gather.3.cloned.1.call-update
  65.6 0.0 all-gather.5.cloned.1.call-start
  65.6 0.1 slice.103
  65.7 0.8 reshape_reshape.7.index_ref
  66.5 0.0 copy-start.1
  66.5 39.8 %shard_map.113 = f32[2560,96]{1,0:T(8,128)} custom-call(s32[38400]{0:T(1024)} %reshape_reshape.7.index_ref, f32[16384,96]{1,0:T(8,128)} %bitcast.73), custom_call_target="tpu_custom_call" | custom-call | tf_op jit(solution)/shard_map/pallas_call | solution.py:32
  106.3 0.0 copy-done.1
  106.3 1.4 multiply_convert_fusion.1
  107.8 0.3 pad_maximum_fusion.9
  108.1 1.5 copy.61
  109.5 21.0 %all_to_all.11 = bf16[8,320,2,96]{1,3,2,0:T(8,128)(2,1)S(1)} all-to-all(bf16[8,320,2,96]{1,3,2,0:T(8,128)(2,1)} %copy.61), channel_id=1, replica_groups=mesh['feat'=8,'dom'=16] {'feat'}, dimensions={0} | all-to-all | bytes 1966080 | tf_op jit(solution)/shard_map/all_to_all | solution.py:87
  130.6 0.0 copy-start.9
  130.6 0.0 copy-start.8
  130.6 4.0 fusion.42
  134.5 0.0 all-gather.5.cloned.1.call-update
  134.5 0.0 all-reduce.3.cloned.1.call-start
  134.6 0.0 copy-done.9
  134.6 0.1 multiply_reduce_fusion
  134.7 0.2 mul.16
  134.9 0.1 copy.62
  135.0 0.2 mul.19
  135.3 0.1 copy.63
  135.4 0.0 copy-done.8
  135.4 0.0 copy-start.3
  135.5 0.0 copy-start.5
  135.5 0.0 copy-start.6
  135.5 10.5 %fusion.29 = bf16[512,3072]{1,0:T(8,128)(2,1)} fusion(s32[512]{0:T(512)S(1)} %bitcast.82, s32[512]{0:T(512)S(1)} %bitcast.83, s32[512]{0:T(512)S(1)} %bitcast.84, s32[512]{0:T(512)S(1)} %bitcast.85, s32[512]{0:T(512)S(1)} %bitcast.86, s32[512]{0:T(512)S(1)} %bitcast.87, s32[512]{0:T(512)S(1)} %bitcast.88, s32[512]{0:T(512)S(1)} %bitcast.89, ...), kind=kLoop, calls=%fused_computation.49 | loop fusion | flops 62914560 | bytes 3166208 | tf_op jit(solution)/shard_map/add | solution.py:96
  146.0 16.6 %fusion.20 = bf16[512,5120]{1,0:T(8,128)(2,1)} fusion(s32[512]{0:T(512)S(1)} %bitcast.92, s32[512]{0:T(512)S(1)} %bitcast.93, s32[512]{0:T(512)S(1)} %bitcast.94, s32[512]{0:T(512)S(1)} %bitcast.95, s32[512]{0:T(512)S(1)} %bitcast.96, s32[512]{0:T(512)S(1)} %bitcast.97, s32[512]{0:T(512)S(1)} %bitcast.98, s32[512]{0:T(512)S(1)} %bitcast.99, ...), kind=kLoop, calls=%fused_computation.40 | loop fusion | flops 104857600 | bytes 5263360 | tf_op jit(solution)/shard_map/add | solution.py:96
  162.6 0.0 copy-done.3
  162.6 0.0 copy-done.5
  162.6 0.0 copy-done.6
  162.6 3.3 fusion.48
  165.9 0.0 all-gather.3.cloned.1.call-done
  165.9 8.5 %fusion.56 = f32[512,1024]{1,0:T(8,128)} fusion(bf16[512,3072]{1,0:T(8,128)(2,1)} %fusion.29, bf16[3072,1024]{1,0:T(8,128)(2,1)} %all-gather.3.cloned.1.call-done), kind=kOutput, calls=%fused_computation.90 | convolution fusion | flops 3221225472 | bytes 11534336 | tf_op jit(solution)/shard_map/dot_general | solution.py:101
  174.4 41.2 %all-gather.5.cloned.1.call-done = bf16[5120,1024]{1,0:T(8,128)(2,1)} async-done(((bf16[320,1024]{1,0:T(8,128)(2,1)}), bf16[5120,1024]{1,0:T(8,128)(2,1)}) %all-gather.5.cloned.1.call-update) | async-done | bytes 10485776 | tf_op jit(solution)/shard_map/all_gather | solution.py:92
  215.6 10.4 %multiply_convert_fusion = bf16[512,1024]{1,0:T(8,128)(2,1)S(1)} fusion(f32[512,1024]{1,0:T(8,128)} %fusion.56, bf16[512,5120]{1,0:T(8,128)(2,1)} %fusion.20, bf16[5120,1024]{1,0:T(8,128)(2,1)} %all-gather.5.cloned.1.call-done), kind=kOutput, calls=%fused_computation.60 | convolution fusion | flops 5370281984 | bytes 18874368 | tf_op jit(solution)/shard_map/dot_general | solution.py:101
  226.1 0.0 copy-done.4
  226.1 3.3 fusion.57
  229.4 0.0 all-reduce.3.cloned.1.call-update
  229.4 0.0 copy-done
  229.4 0.0 copy-start.10
  229.4 2.5 fusion.49
  231.9 0.0 copy-done.10
  231.9 2.3 add_convert_fusion
  234.2 156.5 %all-reduce.3.cloned.1.call-done = (f32[1024,1024]{1,0:T(8,128)}, f32[1024,1024]{1,0:T(8,128)}) async-done(((f32[1024,1024]{1,0:T(8,128)}, f32[1024,1024]{1,0:T(8,128)}), (f32[1024,1024]{1,0:T(8,128)}, f32[1024,1024]{1,0:T(8,128)})) %all-reduce.3.cloned.1.call-update) | async-done | bytes 8388624 | tf_op jit(solution)/shard_map/psum | solution.py:111
  390.7 4.9 %copy.69 = f32[1024,1024]{1,0:T(8,128)} copy(f32[1024,1024]{1,0:T(8,128)} %get-tuple-element.30) | data formatting | bytes 8388608
  395.7 0.0 copy-done.2
  395.7 2.0 copy.70
  (7 shorter events, 0.1 us)
Async XLA Ops:
  7.2 222.2 %copy-start = (bf16[1024,1024]{1,0:T(8,128)(2,1)S(1)}, bf16[1024,1024]{1,0:T(8,128)(2,1)}, u32[]{:S(2)}) copy-start(bf16[1024,1024]{1,0:T(8,128)(2,1)} %param.15) | copy-start | bytes 6291460
  7.2 6.6 %copy-start.7 = (s32[4096,15]{0,1:T(8,128)S(1)}, s32[4096,15]{0,1:T(8,128)}, u32[]{:S(2)}) copy-start(s32[4096,15]{0,1:T(8,128)} %param.10) | copy-start | bytes 737284
  7.2 158.8 %all-gather.3.cloned.1.call-start = ((), (), s32[]{:S(2)}) async-start(), calls=%async_computation.2 | async-start | bytes 6684672 | tf_op jit(solution)/shard_map/all_gather | solution.py:92
  14.7 27.0 %slice-start = ((bf16[96,16384]{1,0:T(8,128)(2,1)}), bf16[96,4096]{1,0:T(8,128)(2,1)S(1)}, s32[]{:S(2)}) async-start(bf16[96,16384]{1,0:T(8,128)(2,1)} %param.9), calls=%async_computation.5 | async-start | bytes 1572864 | tf_op jit(solution)/shard_map/slice | solution.py:71
  65.6 150.1 %all-gather.5.cloned.1.call-start = ((), (), s32[]{:S(2)}) async-start(), calls=%async_computation.3 | async-start | bytes 11141120 | tf_op jit(solution)/shard_map/all_gather | solution.py:92
  66.5 39.8 %copy-start.1 = (bf16[96,4096]{0,1:T(8,128)(2,1)S(1)}, bf16[96,4096]{0,1:T(8,128)(2,1)}, u32[]{:S(2)}) copy-start(bf16[96,4096]{0,1:T(8,128)(2,1)} %copy.58) | copy-start | bytes 2359300
  130.6 4.0 copy-start.9
  130.6 4.8 %copy-start.8 = (s32[512,10]{0,1:T(8,128)S(1)}, s32[512,10]{0,1:T(8,128)}, u32[]{:S(2)}) copy-start(s32[512,10]{0,1:T(8,128)} %param.14) | copy-start | bytes 61444
  134.5 256.2 %all-reduce.3.cloned.1.call-start = ((), (), s32[]{:S(2)}) async-start(), calls=%async_computation.4 | async-start | bytes 16777216 | tf_op jit(solution)/shard_map/psum | solution.py:111
  135.4 27.2 %copy-start.3 = (bf16[512,1024]{1,0:T(8,128)(2,1)S(1)}, bf16[512,1024]{1,0:T(8,128)(2,1)}, u32[]{:S(2)}) copy-start(bf16[512,1024]{1,0:T(8,128)(2,1)} %param.17) | copy-start | bytes 3145732
  135.5 27.2 %copy-start.5 = (bf16[320,1024]{1,0:T(8,128)(2,1)S(1)}, bf16[320,1024]{1,0:T(8,128)(2,1)}, u32[]{:S(2)}) copy-start(bf16[320,1024]{1,0:T(8,128)(2,1)} %fusion.42) | copy-start | bytes 1966084
  135.5 27.1 %copy-start.6 = (bf16[192,1024]{1,0:T(8,128)(2,1)S(1)}, bf16[192,1024]{1,0:T(8,128)(2,1)}, u32[]{:S(2)}) copy-start(bf16[192,1024]{1,0:T(8,128)(2,1)} %fusion.45) | copy-start | bytes 1179652
  215.6 10.4 %copy-start.4 = (bf16[512,1024]{1,0:T(8,128)(2,1)S(1)}, bf16[512,1024]{1,0:T(8,128)(2,1)}, u32[]{:S(2)}) copy-start(bf16[512,1024]{1,0:T(8,128)(2,1)} %param.17) | copy-start | bytes 3145732
  229.4 2.5 copy-start.10
  390.7 4.9 %copy-start.2 = (f32[1024,1024]{1,0:T(8,128)S(1)}, f32[1024,1024]{1,0:T(8,128)}, u32[]{:S(2)}) copy-start(f32[1024,1024]{1,0:T(8,128)} %get-tuple-element.31) | copy-start | bytes 12582916
Sparse Core Ops, SparseCore 0:
  65.7 61.9 all-gather.2
  134.7 80.9 all-gather.4
  229.5 161.1 all-reduce.2

commit v9 on v8

--- a/solution.py
+++ b/solution.py
@@ -12,7 +12,7 @@
     )
 
 
-def gather_sum(table, index, block=512, unroll=16):
+def gather_sum(table, index, block=512, unroll=32):
     fanout, count = index.shape
     rows, width = table.shape
 

time: 405 us -> 404 us (level)
  no operation moved by 1% of the time
where the time goes in v9:
time: 404 us; the launch traced here: 403 us
  waiting for transfers between devices  198 us (49%)
  Pallas kernels  64.6 us (16%)
  blocking collectives  38.9 us (10%)
  matrix products  37.7 us (9%)
  other arithmetic  30.3 us (8%)
  local copies, waits for them, and re-layouts  19.8 us (5%)
  between operations  14 us (3%)
    psum x1, waiting for transfers between devices, shards(): lax.psum((grad_self, grad_neighbour), ('feat', 'dom'))  157 us
    pallas_call x2, Pallas kernels, gather_sum(): pl.pallas_call(kernel, out_shape=jax.ShapeDtypeStruct((count, width), jnp...  64.6 us
    all_gather x2, waiting for transfers between devices, shards(): segment = lax.all_gather(part_out, 'dom', axis=0, tiled=True)  41.2 us
    all_to_all x2, blocking collectives, shards(): arrived = lax.all_to_all(both, 'feat', 0, 0, tiled=True)  38.9 us
    add x2, other arithmetic, shards(): sum(((flat_rows[:, k:k + 1] == table_index).astype(jnp.bfloat16) for k in...  27.1 us
    dot_general x2, matrix products, shards(): term = jnp.dot(counts, segment, preferred_element_type=jnp.float32)  18.9 us
  transfers between devices with their start and end apart: 3, of which 2 were waited for; matrix products, arithmetic and copies ran while one was open for 13% of the time, Pallas kernels for 10%

profile of v9, /device:TPU:1, one launch (start us, length us, event | category | flops | bytes accessed | tf_op | source)
XLA Modules:
  0.0 403.2 jit_solution(8702138002351219156)
XLA Ops:
  7.2 0.0 copy-start
  7.2 0.0 copy-start.7
  7.2 0.0 all-gather.3.cloned.1.call-start
  7.2 6.5 %copy.59 = f32[96,16384]{0,1:T(8,128)} copy(bf16[96,16384]{1,0:T(8,128)(2,1)} %param.9) | data formatting | bytes 9437184 | tf_op jit(solution)/shard_map/transpose | solution.py:69
  13.7 0.0 copy-done.7
  13.7 0.2 copy.66
  13.9 0.7 reshape_reshape.6.index_ref
  14.7 0.0 slice-start
  14.7 25.4 %shard_map.112 = f32[1536,96]{1,0:T(8,128)} custom-call(s32[23040]{0:T(1024)} %reshape_reshape.6.index_ref, f32[16384,96]{1,0:T(8,128)} %bitcast.72), custom_call_target="tpu_custom_call" | custom-call | tf_op jit(solution)/shard_map/pallas_call | solution.py:32
  40.1 1.2 multiply_convert_fusion.2
  41.3 0.0 slice-done
  41.3 1.3 copy.58
  42.6 1.0 slice_bitcast_fusion.1
  43.6 0.2 pad_maximum_fusion.17
  43.8 17.9 %all_to_all.10 = bf16[8,192,2,96]{3,1,2,0:T(8,128)(2,1)S(1)} all-to-all(bf16[8,192,2,96]{3,1,2,0:T(8,128)(2,1)S(1)} %pad_maximum_fusion.17), channel_id=1, replica_groups=mesh['feat'=8,'dom'=16] {'feat'}, dimensions={0} | all-to-all | bytes 1179648 | tf_op jit(solution)/shard_map/all_to_all | solution.py:87
  61.7 3.5 fusion.45
  65.2 0.0 all-gather.3.cloned.1.call-update
  65.2 0.0 all-gather.5.cloned.1.call-start
  65.2 0.1 slice.103
  65.3 0.8 reshape_reshape.7.index_ref
  66.1 0.0 copy-start.1
  66.1 39.1 %shard_map.113 = f32[2560,96]{1,0:T(8,128)} custom-call(s32[38400]{0:T(1024)} %reshape_reshape.7.index_ref, f32[16384,96]{1,0:T(8,128)} %bitcast.73), custom_call_target="tpu_custom_call" | custom-call | tf_op jit(solution)/shard_map/pallas_call | solution.py:32
  105.3 0.0 copy-done.1
  105.3 1.4 multiply_convert_fusion.1
  106.7 0.3 pad_maximum_fusion.9
  107.0 1.5 copy.61
  108.5 21.0 %all_to_all.11 = bf16[8,320,2,96]{1,3,2,0:T(8,128)(2,1)S(1)} all-to-all(bf16[8,320,2,96]{1,3,2,0:T(8,128)(2,1)} %copy.61), channel_id=1, replica_groups=mesh['feat'=8,'dom'=16] {'feat'}, dimensions={0} | all-to-all | bytes 1966080 | tf_op jit(solution)/shard_map/all_to_all | solution.py:87
  129.5 0.0 copy-start.9
  129.5 0.0 copy-start.8
  129.5 4.0 fusion.42
  133.5 0.0 all-gather.5.cloned.1.call-update
  133.5 0.0 all-reduce.3.cloned.1.call-start
  133.6 0.0 copy-done.9
  133.6 0.1 multiply_reduce_fusion
  133.7 0.2 mul.16
  133.9 0.1 copy.62
  134.0 0.2 mul.19
  134.3 0.1 copy.63
  134.4 0.0 copy-done.8
  134.4 0.0 copy-start.3
  134.4 0.0 copy-start.5
  134.4 0.0 copy-start.6
  134.5 10.5 %fusion.29 = bf16[512,3072]{1,0:T(8,128)(2,1)} fusion(s32[512]{0:T(512)S(1)} %bitcast.82, s32[512]{0:T(512)S(1)} %bitcast.83, s32[512]{0:T(512)S(1)} %bitcast.84, s32[512]{0:T(512)S(1)} %bitcast.85, s32[512]{0:T(512)S(1)} %bitcast.86, s32[512]{0:T(512)S(1)} %bitcast.87, s32[512]{0:T(512)S(1)} %bitcast.88, s32[512]{0:T(512)S(1)} %bitcast.89, ...), kind=kLoop, calls=%fused_computation.49 | loop fusion | flops 62914560 | bytes 3166208 | tf_op jit(solution)/shard_map/add | solution.py:96
  144.9 16.6 %fusion.20 = bf16[512,5120]{1,0:T(8,128)(2,1)} fusion(s32[512]{0:T(512)S(1)} %bitcast.92, s32[512]{0:T(512)S(1)} %bitcast.93, s32[512]{0:T(512)S(1)} %bitcast.94, s32[512]{0:T(512)S(1)} %bitcast.95, s32[512]{0:T(512)S(1)} %bitcast.96, s32[512]{0:T(512)S(1)} %bitcast.97, s32[512]{0:T(512)S(1)} %bitcast.98, s32[512]{0:T(512)S(1)} %bitcast.99, ...), kind=kLoop, calls=%fused_computation.40 | loop fusion | flops 104857600 | bytes 5263360 | tf_op jit(solution)/shard_map/add | solution.py:96
  161.6 0.0 copy-done.3
  161.6 0.0 copy-done.5
  161.6 0.0 copy-done.6
  161.6 3.3 fusion.48
  164.9 0.0 all-gather.3.cloned.1.call-done
  164.9 8.5 %fusion.56 = f32[512,1024]{1,0:T(8,128)} fusion(bf16[512,3072]{1,0:T(8,128)(2,1)} %fusion.29, bf16[3072,1024]{1,0:T(8,128)(2,1)} %all-gather.3.cloned.1.call-done), kind=kOutput, calls=%fused_computation.90 | convolution fusion | flops 3221225472 | bytes 11534336 | tf_op jit(solution)/shard_map/dot_general | solution.py:101
  173.4 41.2 %all-gather.5.cloned.1.call-done = bf16[5120,1024]{1,0:T(8,128)(2,1)} async-done(((bf16[320,1024]{1,0:T(8,128)(2,1)}), bf16[5120,1024]{1,0:T(8,128)(2,1)}) %all-gather.5.cloned.1.call-update) | async-done | bytes 10485776 | tf_op jit(solution)/shard_map/all_gather | solution.py:92
  214.6 10.4 %multiply_convert_fusion = bf16[512,1024]{1,0:T(8,128)(2,1)S(1)} fusion(f32[512,1024]{1,0:T(8,128)} %fusion.56, bf16[512,5120]{1,0:T(8,128)(2,1)} %fusion.20, bf16[5120,1024]{1,0:T(8,128)(2,1)} %all-gather.5.cloned.1.call-done), kind=kOutput, calls=%fused_computation.60 | convolution fusion | flops 5370281984 | bytes 18874368 | tf_op jit(solution)/shard_map/dot_general | solution.py:101
  225.1 0.0 copy-done.4
  225.1 3.3 fusion.57
  228.4 0.0 all-reduce.3.cloned.1.call-update
  228.4 0.0 copy-done
  228.4 0.0 copy-start.10
  228.4 2.5 fusion.49
  230.9 0.0 copy-done.10
  230.9 2.3 add_convert_fusion
  233.2 156.6 %all-reduce.3.cloned.1.call-done = (f32[1024,1024]{1,0:T(8,128)}, f32[1024,1024]{1,0:T(8,128)}) async-done(((f32[1024,1024]{1,0:T(8,128)}, f32[1024,1024]{1,0:T(8,128)}), (f32[1024,1024]{1,0:T(8,128)}, f32[1024,1024]{1,0:T(8,128)})) %all-reduce.3.cloned.1.call-update) | async-done | bytes 8388624 | tf_op jit(solution)/shard_map/psum | solution.py:111
  389.8 4.9 %copy.69 = f32[1024,1024]{1,0:T(8,128)} copy(f32[1024,1024]{1,0:T(8,128)} %get-tuple-element.30) | data formatting | bytes 8388608
  394.7 0.0 copy-done.2
  394.7 2.0 copy.70
  (7 shorter events, 0.1 us)
Async XLA Ops:
  7.2 221.3 %copy-start = (bf16[1024,1024]{1,0:T(8,128)(2,1)S(1)}, bf16[1024,1024]{1,0:T(8,128)(2,1)}, u32[]{:S(2)}) copy-start(bf16[1024,1024]{1,0:T(8,128)(2,1)} %param.15) | copy-start | bytes 6291460
  7.2 6.6 %copy-start.7 = (s32[4096,15]{0,1:T(8,128)S(1)}, s32[4096,15]{0,1:T(8,128)}, u32[]{:S(2)}) copy-start(s32[4096,15]{0,1:T(8,128)} %param.10) | copy-start | bytes 737284
  7.2 157.7 %all-gather.3.cloned.1.call-start = ((), (), s32[]{:S(2)}) async-start(), calls=%async_computation.2 | async-start | bytes 6684672 | tf_op jit(solution)/shard_map/all_gather | solution.py:92
  14.7 26.6 %slice-start = ((bf16[96,16384]{1,0:T(8,128)(2,1)}), bf16[96,4096]{1,0:T(8,128)(2,1)S(1)}, s32[]{:S(2)}) async-start(bf16[96,16384]{1,0:T(8,128)(2,1)} %param.9), calls=%async_computation.5 | async-start | bytes 1572864 | tf_op jit(solution)/shard_map/slice | solution.py:71
  65.2 149.5 %all-gather.5.cloned.1.call-start = ((), (), s32[]{:S(2)}) async-start(), calls=%async_computation.3 | async-start | bytes 11141120 | tf_op jit(solution)/shard_map/all_gather | solution.py:92
  66.1 39.1 %copy-start.1 = (bf16[96,4096]{0,1:T(8,128)(2,1)S(1)}, bf16[96,4096]{0,1:T(8,128)(2,1)}, u32[]{:S(2)}) copy-start(bf16[96,4096]{0,1:T(8,128)(2,1)} %copy.58) | copy-start | bytes 2359300
  129.5 4.0 copy-start.9
  129.5 4.8 %copy-start.8 = (s32[512,10]{0,1:T(8,128)S(1)}, s32[512,10]{0,1:T(8,128)}, u32[]{:S(2)}) copy-start(s32[512,10]{0,1:T(8,128)} %param.14) | copy-start | bytes 61444
  133.5 256.2 %all-reduce.3.cloned.1.call-start = ((), (), s32[]{:S(2)}) async-start(), calls=%async_computation.4 | async-start | bytes 16777216 | tf_op jit(solution)/shard_map/psum | solution.py:111
  134.4 27.2 %copy-start.3 = (bf16[512,1024]{1,0:T(8,128)(2,1)S(1)}, bf16[512,1024]{1,0:T(8,128)(2,1)}, u32[]{:S(2)}) copy-start(bf16[512,1024]{1,0:T(8,128)(2,1)} %param.17) | copy-start | bytes 3145732
  134.4 27.2 %copy-start.5 = (bf16[320,1024]{1,0:T(8,128)(2,1)S(1)}, bf16[320,1024]{1,0:T(8,128)(2,1)}, u32[]{:S(2)}) copy-start(bf16[320,1024]{1,0:T(8,128)(2,1)} %fusion.42) | copy-start | bytes 1966084
  134.4 27.1 %copy-start.6 = (bf16[192,1024]{1,0:T(8,128)(2,1)S(1)}, bf16[192,1024]{1,0:T(8,128)(2,1)}, u32[]{:S(2)}) copy-start(bf16[192,1024]{1,0:T(8,128)(2,1)} %fusion.45) | copy-start | bytes 1179652
  214.6 10.4 %copy-start.4 = (bf16[512,1024]{1,0:T(8,128)(2,1)S(1)}, bf16[512,1024]{1,0:T(8,128)(2,1)}, u32[]{:S(2)}) copy-start(bf16[512,1024]{1,0:T(8,128)(2,1)} %param.17) | copy-start | bytes 3145732
  228.4 2.5 copy-start.10
  389.8 4.9 %copy-start.2 = (f32[1024,1024]{1,0:T(8,128)S(1)}, f32[1024,1024]{1,0:T(8,128)}, u32[]{:S(2)}) copy-start(f32[1024,1024]{1,0:T(8,128)} %get-tuple-element.31) | copy-start | bytes 12582916
Sparse Core Ops, SparseCore 0:
  65.3 61.9 all-gather.2
  133.6 80.9 all-gather.4
  228.5 161.1 all-reduce.2

commit v10 on v9

--- a/solution.py
+++ b/solution.py
@@ -12,7 +12,7 @@
     )
 
 
-def gather_sum(table, index, block=512, unroll=32):
+def gather_sum(table, index, block=512, unroll=64):
     fanout, count = index.shape
     rows, width = table.shape
 

time: 404 us -> 403 us (level)
  no operation moved by 1% of the time
where the time goes in v10:
time: 403 us
  waiting for transfers between devices  198 us (49%)
  Pallas kernels  64 us (16%)
  blocking collectives  38.9 us (10%)
  matrix products  37.8 us (9%)
  other arithmetic  30.3 us (8%)
  local copies, waits for them, and re-layouts  19.8 us (5%)
  between operations  14 us (3%)
    psum x1, waiting for transfers between devices, shards(): lax.psum((grad_self, grad_neighbour), ('feat', 'dom'))  157 us
    pallas_call x2, Pallas kernels, gather_sum(): pl.pallas_call(kernel, out_shape=jax.ShapeDtypeStruct((count, width), jnp...  64 us
    all_gather x2, waiting for transfers between devices, shards(): segment = lax.all_gather(part_out, 'dom', axis=0, tiled=True)  41.1 us
    all_to_all x2, blocking collectives, shards(): arrived = lax.all_to_all(both, 'feat', 0, 0, tiled=True)  38.9 us
    add x2, other arithmetic, shards(): sum(((flat_rows[:, k:k + 1] == table_index).astype(jnp.bfloat16) for k in...  27.1 us
    dot_general x2, matrix products, shards(): term = jnp.dot(counts, segment, preferred_element_type=jnp.float32)  18.9 us
  transfers between devices with their start and end apart: 3, of which 2 were waited for; matrix products, arithmetic and copies ran while one was open for 13% of the time, Pallas kernels for 10%

profile of v10, /device:TPU:1, one launch (start us, length us, event | category | flops | bytes accessed | tf_op | source)
XLA Modules:
  0.0 402.7 jit_solution(10875058861997703748)
XLA Ops:
  7.2 0.0 copy-start
  7.2 0.0 copy-start.7
  7.2 0.0 all-gather.3.cloned.1.call-start
  7.2 6.5 %copy.59 = f32[96,16384]{0,1:T(8,128)} copy(bf16[96,16384]{1,0:T(8,128)(2,1)} %param.9) | data formatting | bytes 9437184 | tf_op jit(solution)/shard_map/transpose | solution.py:69
  13.7 0.0 copy-done.7
  13.7 0.2 copy.66
  13.9 0.7 reshape_reshape.6.index_ref
  14.7 0.0 slice-start
  14.7 25.2 %shard_map.112 = f32[1536,96]{1,0:T(8,128)} custom-call(s32[23040]{0:T(1024)} %reshape_reshape.6.index_ref, f32[16384,96]{1,0:T(8,128)} %bitcast.72), custom_call_target="tpu_custom_call" | custom-call | tf_op jit(solution)/shard_map/pallas_call | solution.py:32
  39.9 1.2 multiply_convert_fusion.2
  41.1 0.0 slice-done
  41.1 1.3 copy.58
  42.4 1.0 slice_bitcast_fusion.1
  43.4 0.2 pad_maximum_fusion.17
  43.6 17.9 %all_to_all.10 = bf16[8,192,2,96]{3,1,2,0:T(8,128)(2,1)S(1)} all-to-all(bf16[8,192,2,96]{3,1,2,0:T(8,128)(2,1)S(1)} %pad_maximum_fusion.17), channel_id=1, replica_groups=mesh['feat'=8,'dom'=16] {'feat'}, dimensions={0} | all-to-all | bytes 1179648 | tf_op jit(solution)/shard_map/all_to_all | solution.py:87
  61.5 3.5 fusion.45
  65.0 0.0 all-gather.3.cloned.1.call-update
  65.0 0.0 all-gather.5.cloned.1.call-start
  65.1 0.1 slice.103
  65.2 0.8 reshape_reshape.7.index_ref
  66.0 0.0 copy-start.1
  66.0 38.8 %shard_map.113 = f32[2560,96]{1,0:T(8,128)} custom-call(s32[38400]{0:T(1024)} %reshape_reshape.7.index_ref, f32[16384,96]{1,0:T(8,128)} %bitcast.73), custom_call_target="tpu_custom_call" | custom-call | tf_op jit(solution)/shard_map/pallas_call | solution.py:32
  104.8 0.0 copy-done.1
  104.8 1.4 multiply_convert_fusion.1
  106.3 0.3 pad_maximum_fusion.9
  106.6 1.5 copy.61
  108.0 21.0 %all_to_all.11 = bf16[8,320,2,96]{1,3,2,0:T(8,128)(2,1)S(1)} all-to-all(bf16[8,320,2,96]{1,3,2,0:T(8,128)(2,1)} %copy.61), channel_id=1, replica_groups=mesh['feat'=8,'dom'=16] {'feat'}, dimensions={0} | all-to-all | bytes 1966080 | tf_op jit(solution)/shard_map/all_to_all | solution.py:87
  129.1 0.0 copy-start.9
  129.1 0.0 copy-start.8
  129.1 4.0 fusion.42
  133.0 0.0 all-gather.5.cloned.1.call-update
  133.1 0.0 all-reduce.3.cloned.1.call-start
  133.1 0.0 copy-done.9
  133.1 0.1 multiply_reduce_fusion
  133.2 0.2 mul.16
  133.4 0.1 copy.62
  133.6 0.2 mul.19
  133.8 0.1 copy.63
  133.9 0.0 copy-done.8
  134.0 0.0 copy-start.3
  134.0 0.0 copy-start.5
  134.0 0.0 copy-start.6
  134.0 10.5 %fusion.29 = bf16[512,3072]{1,0:T(8,128)(2,1)} fusion(s32[512]{0:T(512)S(1)} %bitcast.82, s32[512]{0:T(512)S(1)} %bitcast.83, s32[512]{0:T(512)S(1)} %bitcast.84, s32[512]{0:T(512)S(1)} %bitcast.85, s32[512]{0:T(512)S(1)} %bitcast.86, s32[512]{0:T(512)S(1)} %bitcast.87, s32[512]{0:T(512)S(1)} %bitcast.88, s32[512]{0:T(512)S(1)} %bitcast.89, ...), kind=kLoop, calls=%fused_computation.49 | loop fusion | flops 62914560 | bytes 3166208 | tf_op jit(solution)/shard_map/add | solution.py:96
  144.5 16.6 %fusion.20 = bf16[512,5120]{1,0:T(8,128)(2,1)} fusion(s32[512]{0:T(512)S(1)} %bitcast.92, s32[512]{0:T(512)S(1)} %bitcast.93, s32[512]{0:T(512)S(1)} %bitcast.94, s32[512]{0:T(512)S(1)} %bitcast.95, s32[512]{0:T(512)S(1)} %bitcast.96, s32[512]{0:T(512)S(1)} %bitcast.97, s32[512]{0:T(512)S(1)} %bitcast.98, s32[512]{0:T(512)S(1)} %bitcast.99, ...), kind=kLoop, calls=%fused_computation.40 | loop fusion | flops 104857600 | bytes 5263360 | tf_op jit(solution)/shard_map/add | solution.py:96
  161.1 0.0 copy-done.3
  161.1 0.0 copy-done.5
  161.1 0.0 copy-done.6
  161.1 3.3 fusion.48
  164.5 8.5 %fusion.56 = f32[512,1024]{1,0:T(8,128)} fusion(bf16[512,3072]{1,0:T(8,128)(2,1)} %fusion.29, bf16[3072,1024]{1,0:T(8,128)(2,1)} %all-gather.3.cloned.1.call-done), kind=kOutput, calls=%fused_computation.90 | convolution fusion | flops 3221225472 | bytes 11534336 | tf_op jit(solution)/shard_map/dot_general | solution.py:101
  173.0 41.1 %all-gather.5.cloned.1.call-done = bf16[5120,1024]{1,0:T(8,128)(2,1)} async-done(((bf16[320,1024]{1,0:T(8,128)(2,1)}), bf16[5120,1024]{1,0:T(8,128)(2,1)}) %all-gather.5.cloned.1.call-update) | async-done | bytes 10485776 | tf_op jit(solution)/shard_map/all_gather | solution.py:92
  214.1 0.0 copy-start.4
  214.1 10.4 %multiply_convert_fusion = bf16[512,1024]{1,0:T(8,128)(2,1)S(1)} fusion(f32[512,1024]{1,0:T(8,128)} %fusion.56, bf16[512,5120]{1,0:T(8,128)(2,1)} %fusion.20, bf16[5120,1024]{1,0:T(8,128)(2,1)} %all-gather.5.cloned.1.call-done), kind=kOutput, calls=%fused_computation.60 | convolution fusion | flops 5370281984 | bytes 18874368 | tf_op jit(solution)/shard_map/dot_general | solution.py:101
  224.5 0.0 copy-done.4
  224.6 3.3 fusion.57
  227.9 0.0 all-reduce.3.cloned.1.call-update
  227.9 0.0 copy-done
  227.9 0.0 copy-start.10
  227.9 2.5 fusion.49
  230.4 0.0 copy-done.10
  230.4 2.3 add_convert_fusion
  232.7 156.5 %all-reduce.3.cloned.1.call-done = (f32[1024,1024]{1,0:T(8,128)}, f32[1024,1024]{1,0:T(8,128)}) async-done(((f32[1024,1024]{1,0:T(8,128)}, f32[1024,1024]{1,0:T(8,128)}), (f32[1024,1024]{1,0:T(8,128)}, f32[1024,1024]{1,0:T(8,128)})) %all-reduce.3.cloned.1.call-update) | async-done | bytes 8388624 | tf_op jit(solution)/shard_map/psum | solution.py:111
  389.2 4.9 %copy.69 = f32[1024,1024]{1,0:T(8,128)} copy(f32[1024,1024]{1,0:T(8,128)} %get-tuple-element.30) | data formatting | bytes 8388608
  394.1 0.0 copy-done.2
  394.1 2.0 copy.70
  (7 shorter events, 0.1 us)
Async XLA Ops:
  7.2 220.7 %copy-start = (bf16[1024,1024]{1,0:T(8,128)(2,1)S(1)}, bf16[1024,1024]{1,0:T(8,128)(2,1)}, u32[]{:S(2)}) copy-start(bf16[1024,1024]{1,0:T(8,128)(2,1)} %param.15) | copy-start | bytes 6291460
  7.2 6.6 %copy-start.7 = (s32[4096,15]{0,1:T(8,128)S(1)}, s32[4096,15]{0,1:T(8,128)}, u32[]{:S(2)}) copy-start(s32[4096,15]{0,1:T(8,128)} %param.10) | copy-start | bytes 737284
  7.2 157.3 %all-gather.3.cloned.1.call-start = ((), (), s32[]{:S(2)}) async-start(), calls=%async_computation.2 | async-start | bytes 6684672 | tf_op jit(solution)/shard_map/all_gather | solution.py:92
  14.7 26.4 %slice-start = ((bf16[96,16384]{1,0:T(8,128)(2,1)}), bf16[96,4096]{1,0:T(8,128)(2,1)S(1)}, s32[]{:S(2)}) async-start(bf16[96,16384]{1,0:T(8,128)(2,1)} %param.9), calls=%async_computation.5 | async-start | bytes 1572864 | tf_op jit(solution)/shard_map/slice | solution.py:71
  65.0 149.1 %all-gather.5.cloned.1.call-start = ((), (), s32[]{:S(2)}) async-start(), calls=%async_computation.3 | async-start | bytes 11141120 | tf_op jit(solution)/shard_map/all_gather | solution.py:92
  66.0 38.8 %copy-start.1 = (bf16[96,4096]{0,1:T(8,128)(2,1)S(1)}, bf16[96,4096]{0,1:T(8,128)(2,1)}, u32[]{:S(2)}) copy-start(bf16[96,4096]{0,1:T(8,128)(2,1)} %copy.58) | copy-start | bytes 2359300
  129.1 4.0 %copy-start.9 = (s32[5120,1]{0,1:T(1,128)S(1)}, s32[5120,1]{0,1:T(1,128)}, u32[]{:S(2)}) copy-start(s32[5120,1]{0,1:T(1,128)} %param.13) | copy-start | bytes 61444
  129.1 4.8 %copy-start.8 = (s32[512,10]{0,1:T(8,128)S(1)}, s32[512,10]{0,1:T(8,128)}, u32[]{:S(2)}) copy-start(s32[512,10]{0,1:T(8,128)} %param.14) | copy-start | bytes 61444
  133.1 256.1 %all-reduce.3.cloned.1.call-start = ((), (), s32[]{:S(2)}) async-start(), calls=%async_computation.4 | async-start | bytes 16777216 | tf_op jit(solution)/shard_map/psum | solution.py:111
  134.0 27.2 %copy-start.3 = (bf16[512,1024]{1,0:T(8,128)(2,1)S(1)}, bf16[512,1024]{1,0:T(8,128)(2,1)}, u32[]{:S(2)}) copy-start(bf16[512,1024]{1,0:T(8,128)(2,1)} %param.17) | copy-start | bytes 3145732
  134.0 27.2 %copy-start.5 = (bf16[320,1024]{1,0:T(8,128)(2,1)S(1)}, bf16[320,1024]{1,0:T(8,128)(2,1)}, u32[]{:S(2)}) copy-start(bf16[320,1024]{1,0:T(8,128)(2,1)} %fusion.42) | copy-start | bytes 1966084
  134.0 27.1 %copy-start.6 = (bf16[192,1024]{1,0:T(8,128)(2,1)S(1)}, bf16[192,1024]{1,0:T(8,128)(2,1)}, u32[]{:S(2)}) copy-start(bf16[192,1024]{1,0:T(8,128)(2,1)} %fusion.45) | copy-start | bytes 1179652
  214.1 10.4 %copy-start.4 = (bf16[512,1024]{1,0:T(8,128)(2,1)S(1)}, bf16[512,1024]{1,0:T(8,128)(2,1)}, u32[]{:S(2)}) copy-start(bf16[512,1024]{1,0:T(8,128)(2,1)} %param.17) | copy-start | bytes 3145732
  227.9 2.5 copy-start.10
  389.2 4.9 %copy-start.2 = (f32[1024,1024]{1,0:T(8,128)S(1)}, f32[1024,1024]{1,0:T(8,128)}, u32[]{:S(2)}) copy-start(f32[1024,1024]{1,0:T(8,128)} %get-tuple-element.31) | copy-start | bytes 12582916
Sparse Core Ops, SparseCore 0:
  65.1 61.9 all-gather.2
  133.2 80.8 all-gather.4
  228.0 161.1 all-reduce.2
